TPU v7x, 1024 devices: a whole 4x4x32 slice. The times are simulated.
1024 devices in a mesh: fsdp: 64 (over z, y_lo), tp: 16 (over x, y_hi, core).
Axes of the slice: x: 4, y: 4 (y_hi: 2, y_lo: 2; y = y_hi * 2 + y_lo), z: 32, core: 2. Of those that a mesh axis runs over, the one named last changes fastest.
Arguments:
- dout: bfloat16 [16384, 4096], P('fsdp', 'tp'), may hold values from -6 to 6
- w_out: bfloat16 [8192, 4096], P(('tp', 'fsdp')), may hold values from -0.09375 to 0.09375
- y_scan: bfloat16 [16384, 8192], P('fsdp', 'tp'), may hold values from -6 to 6
- z_gate: bfloat16 [16384, 8192], P('fsdp', 'tp'), may hold values from -6 to 6
- x_conv: bfloat16 [16384, 8192], P('fsdp', 'tp'), may hold values from -6 to 6
- du_scan: bfloat16 [16384, 8192], P('fsdp', 'tp'), may hold values from -9 to 9
- conv_w: float32 [4, 8192], P(None, 'tp'), may hold values from -3 to 3
- conv_b: float32 [8192], P('tp'), may hold values from -1 to 1
Outputs:
- d_y: bfloat16 [16384, 8192], P('fsdp', 'tp')
- d_z: bfloat16 [16384, 8192], P('fsdp', 'tp')
- d_x: bfloat16 [16384, 8192], P('fsdp', 'tp')
- d_conv_w: float32 [4, 8192], P(None, 'tp')
- d_conv_b: float32 [8192], P('tp')
All inputs are finite; a program needn't handle non-finite values.
Results may differ from a plain program's by a relative error of at most 0.001.
Values may be sent and summed in bfloat16 or wider, within the bound.
No kernel may reach another device: no remote copies, remote signals or barrier semaphores. Data moves between devices by JAX's collectives and lax.ppermute only.
A program may use at most 32 MiB of HBM per device.

v0:
```python
import jax
import jax.numpy as jnp
from jax import lax
from jax.sharding import PartitionSpec as P

KW = 4


def shifted(block, axis, distance):
    devices = range(lax.axis_size(axis))
    route = [(i - distance, i) for i in devices if i - distance in devices]
    return lax.ppermute(block, axis, route)


def silu_slope(value):
    sig = jax.nn.sigmoid(value)
    return sig * (1.0 + value * (1.0 - sig))


def local(dout, w_out, y_scan, z_gate, x_conv, du_scan, conv_w, conv_b):
    tok_rows = x_conv.shape[0]
    width = x_conv.shape[1]
    prior = shifted(x_conv[tok_rows - (KW - 1) :], "fsdp", 1)
    leading = jnp.stack([x_conv[: KW - 1], du_scan[: KW - 1]])
    later = shifted(leading, "fsdp", -1)
    extended = jnp.concatenate([prior, x_conv, later[0]], 0)
    span = tok_rows + KW - 1
    pre_all = jnp.zeros((span, width), jnp.float32) + conv_b[None, :]
    for k in range(KW):
        pre_all = pre_all + conv_w[k][None, :] * extended[k : k + span]
    arriving = jnp.concatenate([du_scan, later[1]], 0)
    d_pre_all = arriving.astype(jnp.float32) * silu_slope(pre_all)
    d_pre = d_pre_all[:tok_rows]
    grad_x = jnp.zeros((tok_rows, width), jnp.float32)
    taps = []
    for k in range(KW):
        grad_x = grad_x + conv_w[k][None, :] * d_pre_all[KW - 1 - k : KW - 1 - k + tok_rows]
        taps.append(jnp.sum(d_pre * extended[k : k + tok_rows], 0))
    grad_w, grad_b = lax.psum((jnp.stack(taps), jnp.sum(d_pre, 0)), "fsdp")
    full_out = lax.all_gather(dout, "tp", axis=1, tiled=True)
    group_w = lax.all_gather(w_out, "fsdp", axis=0, tiled=True)
    d_gated = lax.dot_general(
        full_out, group_w, (((1,), (1,)), ((), ())), preferred_element_type=jnp.float32
    )
    gate_f = z_gate.astype(jnp.float32)
    grad_y = (d_gated * jax.nn.silu(gate_f)).astype(jnp.bfloat16)
    grad_z = (d_gated * y_scan.astype(jnp.float32) * silu_slope(gate_f)).astype(jnp.bfloat16)
    return (grad_y, grad_z, grad_x.astype(jnp.bfloat16), grad_w, grad_b)


def solution(mesh):
    return jax.shard_map(
        local,
        mesh=mesh,
        in_specs=(
            P("fsdp", "tp"),
            P(("tp", "fsdp"), None),
            P("fsdp", "tp"),
            P("fsdp", "tp"),
            P("fsdp", "tp"),
            P("fsdp", "tp"),
            P(None, "tp"),
            P("tp"),
        ),
        out_specs=(P("fsdp", "tp"), P("fsdp", "tp"), P("fsdp", "tp"), P(None, "tp"), P("tp")),
        check_vma=False,
    )
```

profile of v0, /device:TPU:4, one launch (start us, length us, event | category | flops | bytes accessed | tf_op | source)
XLA Modules:
  0.0 382.3 jit_solution(14533953642166000643)
XLA Ops:
  7.2 0.0 copy-start
  7.2 0.0 copy-start.1
  7.2 0.0 all-gather.3.cloned.1.call-start
  7.2 0.7 all-gather.3.cloned.1.call-update
  7.9 0.0 all-gather.5.cloned.1.call-start
  8.0 0.7 all-gather.5.cloned.1.call-update
  8.7 0.7 slice_bitcast_fusion.3
  9.4 3.5 collective-permute-start.1
  12.9 0.7 slice_bitcast_fusion.2
  13.6 1.3 collective-permute-start
  14.9 0.9 fusion.16
  15.7 3.4 collective-permute-done
  19.1 0.0 collective-permute-done.1
  19.1 1.0 pad_maximum_fusion.1
  20.2 1.7 multiply_multiply_fusion
  21.8 2.8 multiply_reduce_fusion.3
  24.6 252.0 %all-reduce = (f32[4,512]{1,0:T(4,128)}, f32[512]{0:T(512)}) all-reduce(f32[4,512]{1,0:T(4,128)S(1)} %pad_maximum_fusion.3, f32[512]{0:T(512)S(1)} %get-tuple-element.9), channel_id=1, replica_groups=mesh['fsdp'=64,'tp'=16] {'fsdp'}, use_global_device_ids=true, to_apply=%region_4.0 | all-reduce | flops 2560 | bytes 20480 | tf_op jit(solution)/shard_map/psum | solution.py:39
  276.7 0.0 all-gather.3.cloned.1.call-done
  276.7 93.8 %all-gather.5.cloned.1.call-done = bf16[512,4096]{1,0:T(8,128)(2,1)} async-done(((bf16[8,4096]{1,0:T(8,128)(2,1)}), bf16[512,4096]{1,0:T(8,128)(2,1)}) %all-gather.5.cloned.1.call-update) | async-done | bytes 4194320 | tf_op jit(solution)/shard_map/all_gather | solution.py:41
  370.4 0.0 copy-done
  370.4 0.0 copy-done.1
  370.4 5.0 %fusion.8 = (bf16[256,512]{1,0:T(8,128)(2,1)}, bf16[256,512]{1,0:T(8,128)(2,1)}) fusion(bf16[256,512]{1,0:T(8,128)(2,1)S(1)} %copy-done, bf16[256,512]{1,0:T(8,128)(2,1)S(1)} %copy-done.1, bf16[256,4096]{1,0:T(8,128)(2,1)} %all-gather.3.cloned.1.call-done, bf16[512,4096]{1,0:T(8,128)(2,1)} %all-gather.5.cloned.1.call-done), kind=kOutput, calls=%fused_computation.16 | convolution fusion | flops 1075707904 | bytes 7340032 | tf_op jit(solution)/shard_map/dot_general | solution.py:42
  (3 shorter events, 0.0 us)
Async XLA Ops:
  7.2 363.3 %copy-start = (bf16[256,512]{1,0:T(8,128)(2,1)S(1)}, bf16[256,512]{1,0:T(8,128)(2,1)}, u32[]{:S(2)}) copy-start(bf16[256,512]{1,0:T(8,128)(2,1)} %param.11) | copy-start | bytes 786436
  7.2 363.3 %copy-start.1 = (bf16[256,512]{1,0:T(8,128)(2,1)S(1)}, bf16[256,512]{1,0:T(8,128)(2,1)}, u32[]{:S(2)}) copy-start(bf16[256,512]{1,0:T(8,128)(2,1)} %param.10) | copy-start | bytes 786436
  7.2 269.5 %all-gather.3.cloned.1.call-start = ((), (), s32[]{:S(2)}) async-start(), calls=%async_computation | async-start | bytes 2228224 | tf_op jit(solution)/shard_map/all_gather | solution.py:40
  7.9 362.5 %all-gather.5.cloned.1.call-start = ((), (), s32[]{:S(2)}) async-start(), calls=%async_computation.1 | async-start | bytes 4259840 | tf_op jit(solution)/shard_map/all_gather | solution.py:41
  9.4 9.7 %collective-permute-start.1 = (bf16[3,512]{1,0:T(4,128)(2,1)S(1)}, bf16[3,512]{1,0:T(4,128)(2,1)S(1)}, u32[]{:S(2)}, u32[]{:S(2)}) collective-permute-start(bf16[3,512]{1,0:T(4,128)(2,1)S(1)} %get-tuple-element.16), channel_id=1, source_target_pairs={{0,16},{16,32},{32,48},{48,64},{64,80},{80,96},{96,112},{112,128},... | collective-permute-start | bytes 9224 | tf_op jit(solution)/shard_map/ppermute | solution.py:12
  13.6 5.5 %collective-permute-start = (bf16[2,3,512]{2,1,0:T(4,128)(2,1)S(1)}, bf16[2,3,512]{2,1,0:T(4,128)(2,1)S(1)}, u32[]{:S(2)}, u32[]{:S(2)}) collective-permute-start(bf16[2,3,512]{2,1,0:T(4,128)(2,1)S(1)} %pad_maximum_fusion.2), channel_id=1, source_target_pairs={{16,0},{32,16},{48,32},{64,48},{80,64},{96,80},{112,96},{128,112},... | collective-permute-start | bytes 18440 | tf_op jit(solution)/shard_map/ppermute | solution.py:12
Sparse Core Ops, SparseCore 0:
  12.3 91.8 all-gather.2
  106.9 263.5 all-gather.4
where the time goes:
time: 383 us; the launch traced here: 382 us
  blocking collectives  252 us (66%)
  waiting for transfers between devices  98.6 us (26%)
  between operations  14.1 us (4%)
  other arithmetic  5.48 us (1%)
  matrix products  5.04 us (1%)
  starting transfers between devices  4.84 us (1%)
    psum x1, blocking collectives, local(): grad_w, grad_b = lax.psum((jnp.stack(taps), jnp.sum(d_pre, 0)), 'fsdp')  252 us
    all_gather x1, waiting for transfers between devices, local(): group_w = lax.all_gather(w_out, 'fsdp', axis=0, tiled=True)  93.8 us
  transfers between devices with their start and end apart: 4, of which 2 were waited for; matrix products, arithmetic and copies ran while one was open for 2% of the time, Pallas kernels for 0%

commit v1 on v0

v1 whole, which is shorter than its diff:
```python
import jax
import jax.numpy as jnp
from jax import lax
from jax.sharding import Mesh
from jax.sharding import PartitionSpec as P

KW = 4
FSDP = ("zh", "zl", "ylo")


def shifted(block, axis, distance):
    devices = range(lax.axis_size(axis))
    route = [(i - distance, i) for i in devices if i - distance in devices]
    return lax.ppermute(block, axis, route)


def silu_slope(value):
    sig = jax.nn.sigmoid(value)
    return sig * (1.0 + value * (1.0 - sig))


def butterfly_sum(value, axis, bits):
    n = lax.axis_size(axis)
    for b in bits:
        value = value + lax.ppermute(value, axis, [(i, i ^ (1 << b)) for i in range(n)])
    return value


def butterfly_gather(block, axis, bits):
    n = lax.axis_size(axis)
    me = lax.axis_index(axis)
    buf = block[None]
    for b in bits:
        recv = lax.ppermute(buf, axis, [(i, i ^ (1 << b)) for i in range(n)])
        bit = (me >> b) & 1
        pair = jnp.zeros((2,) + buf.shape, buf.dtype)
        pair = lax.dynamic_update_slice(pair, buf[None], (bit,) + (0,) * buf.ndim)
        pair = lax.dynamic_update_slice(pair, recv[None], (1 - bit,) + (0,) * buf.ndim)
        buf = pair
    k = len(bits)
    buf = buf.reshape(buf.shape[:k] + block.shape)
    held = [bits[k - 1 - j] for j in range(k)]
    order = sorted(range(k), key=lambda j: -held[j])
    buf = jnp.transpose(buf, order + list(range(k, k + block.ndim)))
    return buf.reshape((n,) + block.shape)


def local(dout, w_out, y_scan, z_gate, x_conv, du_scan, conv_w, conv_b):
    tok_rows = x_conv.shape[0]
    width = x_conv.shape[1]
    prior = shifted(x_conv[tok_rows - (KW - 1) :], FSDP, 1)
    leading = jnp.stack([x_conv[: KW - 1], du_scan[: KW - 1]])
    later = shifted(leading, FSDP, -1)
    extended = jnp.concatenate([prior, x_conv, later[0]], 0)
    span = tok_rows + KW - 1
    pre_all = jnp.zeros((span, width), jnp.float32) + conv_b[None, :]
    for k in range(KW):
        pre_all = pre_all + conv_w[k][None, :] * extended[k : k + span]
    arriving = jnp.concatenate([du_scan, later[1]], 0)
    d_pre_all = arriving.astype(jnp.float32) * silu_slope(pre_all)
    d_pre = d_pre_all[:tok_rows]
    grad_x = jnp.zeros((tok_rows, width), jnp.float32)
    taps = []
    for k in range(KW):
        grad_x = grad_x + conv_w[k][None, :] * d_pre_all[KW - 1 - k : KW - 1 - k + tok_rows]
        taps.append(jnp.sum(d_pre * extended[k : k + tok_rows], 0))
    partial = jnp.concatenate([jnp.stack(taps), jnp.sum(d_pre, 0)[None]], 0)
    fsdp_bits = (lax.axis_size(FSDP) - 1).bit_length()
    total = butterfly_sum(partial, FSDP, list(range(fsdp_bits)))
    grad_w, grad_b = total[:KW], total[KW]
    tp_bits = (lax.axis_size("tp") - 1).bit_length()
    out_blocks = butterfly_gather(dout, "tp", [1] + list(range(tp_bits - 1, 1, -1)) + [0])
    group_w = lax.all_gather(w_out, "ylo", axis=0, tiled=True)
    group_w = lax.all_gather(group_w, "zl", axis=0, tiled=True)
    group_w = lax.all_gather(group_w, "zh", axis=0, tiled=True)
    n_tp = out_blocks.shape[0]
    w_blocks = group_w.reshape(group_w.shape[0], n_tp, dout.shape[1])
    d_gated = lax.dot_general(
        out_blocks, w_blocks, (((0, 2), (1, 2)), ((), ())), preferred_element_type=jnp.float32
    )
    gate_f = z_gate.astype(jnp.float32)
    grad_y = (d_gated * jax.nn.silu(gate_f)).astype(jnp.bfloat16)
    grad_z = (d_gated * y_scan.astype(jnp.float32) * silu_slope(gate_f)).astype(jnp.bfloat16)
    return (grad_y, grad_z, grad_x.astype(jnp.bfloat16), grad_w, grad_b)


def solution(mesh):
    n_f = mesh.shape["fsdp"]
    n_t = mesh.shape["tp"]
    view = Mesh(mesh.devices.reshape(n_f // 4, 2, 2, n_t), FSDP + ("tp",))
    tok = P(FSDP, "tp")
    return jax.shard_map(
        local,
        mesh=view,
        in_specs=(
            tok,
            P(("tp",) + FSDP, None),
            tok,
            tok,
            tok,
            tok,
            P(None, "tp"),
            P("tp"),
        ),
        out_specs=(tok, tok, tok, P(None, "tp"), P("tp")),
        check_vma=False,
    )
```

time: 383 us -> 178 us (0.46)
  the two profiles are of different devices: /device:TPU:4 before, /device:TPU:2 now
where the time goes in v1:
time: 178 us; the launch traced here: 177 us
  waiting for transfers between devices  67.2 us (38%)
  starting transfers between devices  66.1 us (37%)
  between operations  14.4 us (8%)
  local copies, waits for them, and re-layouts  12 us (7%)
  blocking collectives  10.9 us (6%)
  matrix products  4.35 us (2%)
  other arithmetic  1.8 us (1%)
    ppermute x6, starting transfers between devices, butterfly_sum(): lax.ppermute(value, axis, [(i, i ^ 1 << b) for i in range(n)])  36.9 us
    ppermute x6, waiting for transfers between devices, butterfly_sum(): lax.ppermute(value, axis, [(i, i ^ 1 << b) for i in range(n)])  35.2 us
    ppermute x4, starting transfers between devices, butterfly_gather(): recv = lax.ppermute(buf, axis, [(i, i ^ 1 << b) for i in range(n)])  25.3 us
    all_gather x1, waiting for transfers between devices, local(): group_w = lax.all_gather(group_w, 'zh', axis=0, tiled=True)  21.4 us
    ppermute x4, waiting for transfers between devices, butterfly_gather(): recv = lax.ppermute(buf, axis, [(i, i ^ 1 << b) for i in range(n)])  10.6 us
    all_gather x1, local copies, waits for them, and re-layouts, local(): group_w = lax.all_gather(group_w, 'zh', axis=0, tiled=True)  6.49 us
    all_gather x1, blocking collectives, local(): group_w = lax.all_gather(group_w, 'zl', axis=0, tiled=True)  5.74 us
    all_gather x1, blocking collectives, local(): group_w = lax.all_gather(w_out, 'ylo', axis=0, tiled=True)  5.15 us
  transfers between devices with their start and end apart: 13, of which 9 were waited for; matrix products, arithmetic and copies ran while one was open for 4% of the time, Pallas kernels for 0%

profile of v1, /device:TPU:2, one launch (start us, length us, event | category | flops | bytes accessed | tf_op | source)
XLA Modules:
  0.0 176.8 jit_solution(5824380331833215851)
XLA Ops:
  7.2 5.2 %all_gather.9 = bf16[16,4096]{1,0:T(8,128)(2,1)S(1)} all-gather(bf16[8,4096]{1,0:T(8,128)(2,1)} %param.9), channel_id=1, replica_groups=mesh['zh'=16,'zl'=2,'ylo'=2,'tp'=16] {'ylo'}, dimensions={0}, use_global_device_ids=true | all-gather | bytes 196608 | tf_op jit(solution)/shard_map/all_gather | solution.py:73
  12.4 5.7 %all_gather.10 = bf16[32,4096]{1,0:T(8,128)(2,1)} all-gather(bf16[16,4096]{1,0:T(8,128)(2,1)S(1)} %all_gather.9), channel_id=1, replica_groups=mesh['zh'=16,'zl'=2,'ylo'=2,'tp'=16] {'zl'}, dimensions={0}, use_global_device_ids=true | all-gather | bytes 393216 | tf_op jit(solution)/shard_map/all_gather | solution.py:74
  18.1 5.1 %collective-permute-start = (bf16[1,256,256]{2,1,0:T(8,128)(2,1)}, bf16[1,256,256]{2,1,0:T(8,128)(2,1)S(1)}, u32[]{:S(2)}, u32[]{:S(2)}) collective-permute-start(bf16[1,256,256]{2,1,0:T(8,128)(2,1)} %bitcast.49), channel_id=1, source_target_pairs={{0,2},{1,3},{2,0},{3,1},{4,6},{5,7},{6,4},{7,5},{8,10},{9,11},{10,... | collective-permute-start | bytes 393224 | tf_op jit(solution)/shard_map/ppermute | solution.py:34
  23.3 0.7 slice_bitcast_fusion.3
  24.0 2.6 %collective-permute-start.5 = (bf16[3,512]{1,0:T(4,128)(2,1)S(1)}, bf16[3,512]{1,0:T(4,128)(2,1)S(1)}, u32[]{:S(2)}, u32[]{:S(2)}) collective-permute-start(bf16[3,512]{1,0:T(4,128)(2,1)S(1)} %get-tuple-element.14), channel_id=1, source_target_pairs={{0,16},{16,32},{32,48},{48,64},{64,80},{80,96},{96,112},{112,128},... | collective-permute-start | bytes 9224 | tf_op jit(solution)/shard_map/ppermute | solution.py:14
  26.6 0.9 bitcast_dynamic-update-slice_fusion.7
  27.6 4.0 %collective-permute-start.1 = (bf16[2,1,256,256]{3,2,1,0:T(8,128)(2,1)S(1)}, bf16[2,1,256,256]{3,2,1,0:T(8,128)(2,1)S(1)}, u32[]{:S(2)}, u32[]{:S(2)}) collective-permute-start(bf16[2,1,256,256]{3,2,1,0:T(8,128)(2,1)S(1)} %bitcast_dynamic-update-slice_fusion.6), channel_id=1, source_target_pairs={{0,8},{1,9},{2,10},{3,11},{4,12},{5,13},{6,14},{7,15},{8,0},{9,1},... | collective-permute-start | bytes 786440 | tf_op jit(solution)/shard_map/ppermute | solution.py:34
  31.6 0.7 slice_bitcast_fusion.2
  32.4 4.9 %collective-permute-done.1 = bf16[2,1,256,256]{3,2,1,0:T(8,128)(2,1)S(1)} collective-permute-done((bf16[2,1,256,256]{3,2,1,0:T(8,128)(2,1)S(1)}, bf16[2,1,256,256]{3,2,1,0:T(8,128)(2,1)S(1)}, u32[]{:S(2)}, u32[]{:S(2)}) %collective-permute-start.1) | collective-permute-done | bytes 262176 | tf_op jit(solution)/shard_map/ppermute | solution.py:34
  37.3 14.3 %collective-permute-start.2 = (bf16[2,2,1,256,256]{4,3,1,0,2:T(8,128)(2,1)S(1)}, bf16[2,2,1,256,256]{4,3,1,0,2:T(8,128)(2,1)S(1)}, u32[]{:S(2)}, u32[]{:S(2)}) collective-permute-start(bf16[2,2,1,256,256]{4,3,1,0,2:T(8,128)(2,1)S(1)} %bitcast_dynamic-update-slice_fusion.4), channel_id=1, source_target_pairs={{0,4},{1,5},{2,6},{3,7},{4,0},{5,1},{6,2},{7,3},{8,12},{9,13},{10,... | collective-permute-start | bytes 1572872 | tf_op jit(solution)/shard_map/ppermute | solution.py:34
  51.6 1.3 collective-permute-start.4
  53.1 5.7 %collective-permute-done.2 = bf16[2,2,1,256,256]{4,3,1,0,2:T(8,128)(2,1)S(1)} collective-permute-done((bf16[2,2,1,256,256]{4,3,1,0,2:T(8,128)(2,1)S(1)}, bf16[2,2,1,256,256]{4,3,1,0,2:T(8,128)(2,1)S(1)}, u32[]{:S(2)}, u32[]{:S(2)}) %collective-permute-start.2) | collective-permute-done | bytes 524320 | tf_op jit(solution)/shard_map/ppermute | solution.py:34
  58.8 1.9 %collective-permute-start.3 = (bf16[2,2,2,1,256,256]{5,4,2,0,1,3:T(8,128)(2,1)S(1)}, bf16[2,2,2,1,256,256]{5,4,2,0,1,3:T(8,128)(2,1)}, u32[]{:S(2)}, u32[]{:S(2)}) collective-permute-start(bf16[2,2,2,1,256,256]{5,4,2,0,1,3:T(8,128)(2,1)S(1)} %bitcast_dynamic-update-slice_fusion.3), channel_id=1, source_target_pairs={{0,1},{1,0},{2,3},{3,2},{4,5},{5,4},{6,7},{7,6},{8,9},{9,8},{10,11... | collective-permute-start | bytes 3145736 | tf_op jit(solution)/shard_map/ppermute | solution.py:34
  61.4 1.2 multiply_reduce_fusion.1
  62.6 3.7 %collective-permute-start.6 = (f32[5,512]{1,0:T(8,128)S(1)}, f32[5,512]{1,0:T(8,128)S(1)}, u32[]{:S(2)}, u32[]{:S(2)}) collective-permute-start(f32[5,512]{1,0:T(8,128)S(1)} %concatenate.22), channel_id=1, source_target_pairs={{0,16},{16,0},{32,48},{48,32},{64,80},{80,64},{96,112},{112,96},{1... | collective-permute-start | bytes 30728 | tf_op jit(solution)/shard_map/ppermute | solution.py:25
  66.4 1.9 %collective-permute-done.6 = f32[5,512]{1,0:T(8,128)S(1)} collective-permute-done((f32[5,512]{1,0:T(8,128)S(1)}, f32[5,512]{1,0:T(8,128)S(1)}, u32[]{:S(2)}, u32[]{:S(2)}) %collective-permute-start.6) | collective-permute-done | bytes 10272 | tf_op jit(solution)/shard_map/ppermute | solution.py:25
  68.3 3.4 %collective-permute-start.7 = (f32[5,512]{1,0:T(8,128)S(1)}, f32[5,512]{1,0:T(8,128)S(1)}, u32[]{:S(2)}, u32[]{:S(2)}) collective-permute-start(f32[5,512]{1,0:T(8,128)S(1)} %add.106), channel_id=1, source_target_pairs={{0,32},{16,48},{32,0},{48,16},{64,96},{80,112},{96,64},{112,80},{1... | collective-permute-start | bytes 30728 | tf_op jit(solution)/shard_map/ppermute | solution.py:25
  71.7 2.5 %collective-permute-done.7 = f32[5,512]{1,0:T(8,128)S(1)} collective-permute-done((f32[5,512]{1,0:T(8,128)S(1)}, f32[5,512]{1,0:T(8,128)S(1)}, u32[]{:S(2)}, u32[]{:S(2)}) %collective-permute-start.7) | collective-permute-done | bytes 10272 | tf_op jit(solution)/shard_map/ppermute | solution.py:25
  74.2 1.9 %collective-permute-start.8 = (f32[5,512]{1,0:T(8,128)S(1)}, f32[5,512]{1,0:T(8,128)S(1)}, u32[]{:S(2)}, u32[]{:S(2)}) collective-permute-start(f32[5,512]{1,0:T(8,128)S(1)} %add.107), channel_id=1, source_target_pairs={{0,64},{16,80},{32,96},{48,112},{64,0},{80,16},{96,32},{112,48},{1... | collective-permute-start | bytes 30728 | tf_op jit(solution)/shard_map/ppermute | solution.py:25
  76.1 6.1 %collective-permute-done.8 = f32[5,512]{1,0:T(8,128)S(1)} collective-permute-done((f32[5,512]{1,0:T(8,128)S(1)}, f32[5,512]{1,0:T(8,128)S(1)}, u32[]{:S(2)}, u32[]{:S(2)}) %collective-permute-start.8) | collective-permute-done | bytes 10272 | tf_op jit(solution)/shard_map/ppermute | solution.py:25
  82.2 1.9 %collective-permute-start.9 = (f32[5,512]{1,0:T(8,128)S(1)}, f32[5,512]{1,0:T(8,128)S(1)}, u32[]{:S(2)}, u32[]{:S(2)}) collective-permute-start(f32[5,512]{1,0:T(8,128)S(1)} %add.108), channel_id=1, source_target_pairs={{0,128},{16,144},{32,160},{48,176},{64,192},{80,208},{96,224},{112... | collective-permute-start | bytes 30728 | tf_op jit(solution)/shard_map/ppermute | solution.py:25
  84.1 9.5 %collective-permute-done.9 = f32[5,512]{1,0:T(8,128)S(1)} collective-permute-done((f32[5,512]{1,0:T(8,128)S(1)}, f32[5,512]{1,0:T(8,128)S(1)}, u32[]{:S(2)}, u32[]{:S(2)}) %collective-permute-start.9) | collective-permute-done | bytes 10272 | tf_op jit(solution)/shard_map/ppermute | solution.py:25
  93.6 8.9 %collective-permute-start.10 = (f32[5,512]{1,0:T(8,128)S(1)}, f32[5,512]{1,0:T(8,128)S(1)}, u32[]{:S(2)}, u32[]{:S(2)}) collective-permute-start(f32[5,512]{1,0:T(8,128)S(1)} %add.109), channel_id=1, source_target_pairs={{0,256},{16,272},{32,288},{48,304},{64,320},{80,336},{96,352},{112... | collective-permute-start | bytes 30728 | tf_op jit(solution)/shard_map/ppermute | solution.py:25
  102.5 7.9 %collective-permute-done.10 = f32[5,512]{1,0:T(8,128)S(1)} collective-permute-done((f32[5,512]{1,0:T(8,128)S(1)}, f32[5,512]{1,0:T(8,128)S(1)}, u32[]{:S(2)}, u32[]{:S(2)}) %collective-permute-start.10) | collective-permute-done | bytes 10272 | tf_op jit(solution)/shard_map/ppermute | solution.py:25
  110.4 17.0 %collective-permute-start.11 = (f32[5,512]{1,0:T(8,128)S(1)}, f32[5,512]{1,0:T(8,128)S(1)}, u32[]{:S(2)}, u32[]{:S(2)}) collective-permute-start(f32[5,512]{1,0:T(8,128)S(1)} %add.110), channel_id=1, source_target_pairs={{0,512},{16,528},{32,544},{48,560},{64,576},{80,592},{96,608},{112... | collective-permute-start | bytes 30728 | tf_op jit(solution)/shard_map/ppermute | solution.py:25
  127.4 7.4 %collective-permute-done.11 = f32[5,512]{1,0:T(8,128)S(1)} collective-permute-done((f32[5,512]{1,0:T(8,128)S(1)}, f32[5,512]{1,0:T(8,128)S(1)}, u32[]{:S(2)}, u32[]{:S(2)}) %collective-permute-start.11) | collective-permute-done | bytes 10272 | tf_op jit(solution)/shard_map/ppermute | solution.py:25
  134.8 0.6 slice.106
  135.4 0.6 slice.107
  136.3 1.3 bitcast_dynamic-update-slice_fusion.1
  137.6 21.4 %all-gather.2.cloned.1.call-done = bf16[512,4096]{1,0:T(8,128)(2,1)} async-done(((bf16[32,4096]{1,0:T(8,128)(2,1)}), bf16[512,4096]{1,0:T(8,128)(2,1)}) %all-gather.2.cloned.1.call-update) | async-done | bytes 4194320 | tf_op jit(solution)/shard_map/all_gather | solution.py:75
  159.1 6.5 %copy.21 = bf16[512,4096]{0,1:T(8,128)(2,1)} copy(bf16[512,4096]{1,0:T(8,128)(2,1)} %all-gather.2.cloned.1.call-done) | data formatting | bytes 8388608 | tf_op jit(solution)/shard_map/all_gather | solution.py:75
  165.6 4.4 %fusion.8 = (bf16[256,512]{1,0:T(8,128)(2,1)}, bf16[256,512]{1,0:T(8,128)(2,1)}) fusion(bf16[256,512]{1,0:T(8,128)(2,1)S(1)} %copy-done.4, bf16[256,512]{1,0:T(8,128)(2,1)S(1)} %copy-done.5, bf16[16,256,256]{2,1,0:T(8,128)(2,1)S(1)} %bitcast.48, bf16[512,16,256]{0,2,1:T(8,128)(2,1)} %bitcast.47), kind=kOutput, calls=%fused_computation.19 | convolution fusion | flops 1075707904 | bytes 7340032 | tf_op jit(solution)/shard_map/dot_general | solution.py:78
  (40 shorter events, 1.3 us)
Async XLA Ops:
  7.2 45.8 %copy-start.2 = (f32[4,512]{1,0:T(4,128)S(1)}, f32[4,512]{1,0:T(4,128)}, u32[]{:S(2)}) copy-start(f32[4,512]{1,0:T(4,128)} %param.14) | copy-start | bytes 24580
  7.2 151.9 %all-gather.2.cloned.1.call-start = ((), (), s32[]{:S(2)}) async-start(), calls=%async_computation | async-start | bytes 4456448 | tf_op jit(solution)/shard_map/all_gather | solution.py:75
  18.1 9.4 %collective-permute-start = (bf16[1,256,256]{2,1,0:T(8,128)(2,1)}, bf16[1,256,256]{2,1,0:T(8,128)(2,1)S(1)}, u32[]{:S(2)}, u32[]{:S(2)}) collective-permute-start(bf16[1,256,256]{2,1,0:T(8,128)(2,1)} %bitcast.49), channel_id=1, source_target_pairs={{0,2},{1,3},{2,0},{3,1},{4,6},{5,7},{6,4},{7,5},{8,10},{9,11},{10,... | collective-permute-start | bytes 393224 | tf_op jit(solution)/shard_map/ppermute | solution.py:34
  24.0 36.8 %collective-permute-start.5 = (bf16[3,512]{1,0:T(4,128)(2,1)S(1)}, bf16[3,512]{1,0:T(4,128)(2,1)S(1)}, u32[]{:S(2)}, u32[]{:S(2)}) collective-permute-start(bf16[3,512]{1,0:T(4,128)(2,1)S(1)} %get-tuple-element.14), channel_id=1, source_target_pairs={{0,16},{16,32},{32,48},{48,64},{64,80},{80,96},{96,112},{112,128},... | collective-permute-start | bytes 9224 | tf_op jit(solution)/shard_map/ppermute | solution.py:14
  27.6 9.8 %collective-permute-start.1 = (bf16[2,1,256,256]{3,2,1,0:T(8,128)(2,1)S(1)}, bf16[2,1,256,256]{3,2,1,0:T(8,128)(2,1)S(1)}, u32[]{:S(2)}, u32[]{:S(2)}) collective-permute-start(bf16[2,1,256,256]{3,2,1,0:T(8,128)(2,1)S(1)} %bitcast_dynamic-update-slice_fusion.6), channel_id=1, source_target_pairs={{0,8},{1,9},{2,10},{3,11},{4,12},{5,13},{6,14},{7,15},{8,0},{9,1},... | collective-permute-start | bytes 786440 | tf_op jit(solution)/shard_map/ppermute | solution.py:34
  32.3 28.4 %copy-start = (bf16[256,512]{1,0:T(8,128)(2,1)S(1)}, bf16[256,512]{1,0:T(8,128)(2,1)}, u32[]{:S(2)}) copy-start(bf16[256,512]{1,0:T(8,128)(2,1)} %param.12) | copy-start | bytes 786436
  32.4 28.5 %copy-start.1 = (bf16[256,512]{1,0:T(8,128)(2,1)S(1)}, bf16[256,512]{1,0:T(8,128)(2,1)}, u32[]{:S(2)}) copy-start(bf16[256,512]{1,0:T(8,128)(2,1)} %param.13) | copy-start | bytes 786436
  32.4 28.5 %copy-start.3 = (f32[512]{0:T(512)S(1)}, f32[512]{0:T(512)}, u32[]{:S(2)}) copy-start(f32[512]{0:T(512)} %param.15) | copy-start | bytes 6148
  37.3 21.4 %collective-permute-start.2 = (bf16[2,2,1,256,256]{4,3,1,0,2:T(8,128)(2,1)S(1)}, bf16[2,2,1,256,256]{4,3,1,0,2:T(8,128)(2,1)S(1)}, u32[]{:S(2)}, u32[]{:S(2)}) collective-permute-start(bf16[2,2,1,256,256]{4,3,1,0,2:T(8,128)(2,1)S(1)} %bitcast_dynamic-update-slice_fusion.4), channel_id=1, source_target_pairs={{0,4},{1,5},{2,6},{3,7},{4,0},{5,1},{6,2},{7,3},{8,12},{9,13},{10,... | collective-permute-start | bytes 1572872 | tf_op jit(solution)/shard_map/ppermute | solution.py:34
  51.6 9.1 %collective-permute-start.4 = (bf16[2,3,512]{2,1,0:T(4,128)(2,1)S(1)}, bf16[2,3,512]{2,1,0:T(4,128)(2,1)S(1)}, u32[]{:S(2)}, u32[]{:S(2)}) collective-permute-start(bf16[2,3,512]{2,1,0:T(4,128)(2,1)S(1)} %pad_maximum_fusion.2), channel_id=1, source_target_pairs={{16,0},{32,16},{48,32},{64,48},{80,64},{96,80},{112,96},{128,112},... | collective-permute-start | bytes 18440 | tf_op jit(solution)/shard_map/ppermute | solution.py:14
  58.8 77.5 %collective-permute-start.3 = (bf16[2,2,2,1,256,256]{5,4,2,0,1,3:T(8,128)(2,1)S(1)}, bf16[2,2,2,1,256,256]{5,4,2,0,1,3:T(8,128)(2,1)}, u32[]{:S(2)}, u32[]{:S(2)}) collective-permute-start(bf16[2,2,2,1,256,256]{5,4,2,0,1,3:T(8,128)(2,1)S(1)} %bitcast_dynamic-update-slice_fusion.3), channel_id=1, source_target_pairs={{0,1},{1,0},{2,3},{3,2},{4,5},{5,4},{6,7},{7,6},{8,9},{9,8},{10,11... | collective-permute-start | bytes 3145736 | tf_op jit(solution)/shard_map/ppermute | solution.py:34
  62.6 5.6 %collective-permute-start.6 = (f32[5,512]{1,0:T(8,128)S(1)}, f32[5,512]{1,0:T(8,128)S(1)}, u32[]{:S(2)}, u32[]{:S(2)}) collective-permute-start(f32[5,512]{1,0:T(8,128)S(1)} %concatenate.22), channel_id=1, source_target_pairs={{0,16},{16,0},{32,48},{48,32},{64,80},{80,64},{96,112},{112,96},{1... | collective-permute-start | bytes 30728 | tf_op jit(solution)/shard_map/ppermute | solution.py:25
  68.3 5.9 %collective-permute-start.7 = (f32[5,512]{1,0:T(8,128)S(1)}, f32[5,512]{1,0:T(8,128)S(1)}, u32[]{:S(2)}, u32[]{:S(2)}) collective-permute-start(f32[5,512]{1,0:T(8,128)S(1)} %add.106), channel_id=1, source_target_pairs={{0,32},{16,48},{32,0},{48,16},{64,96},{80,112},{96,64},{112,80},{1... | collective-permute-start | bytes 30728 | tf_op jit(solution)/shard_map/ppermute | solution.py:25
  74.2 8.0 %collective-permute-start.8 = (f32[5,512]{1,0:T(8,128)S(1)}, f32[5,512]{1,0:T(8,128)S(1)}, u32[]{:S(2)}, u32[]{:S(2)}) collective-permute-start(f32[5,512]{1,0:T(8,128)S(1)} %add.107), channel_id=1, source_target_pairs={{0,64},{16,80},{32,96},{48,112},{64,0},{80,16},{96,32},{112,48},{1... | collective-permute-start | bytes 30728 | tf_op jit(solution)/shard_map/ppermute | solution.py:25
  82.2 11.4 %collective-permute-start.9 = (f32[5,512]{1,0:T(8,128)S(1)}, f32[5,512]{1,0:T(8,128)S(1)}, u32[]{:S(2)}, u32[]{:S(2)}) collective-permute-start(f32[5,512]{1,0:T(8,128)S(1)} %add.108), channel_id=1, source_target_pairs={{0,128},{16,144},{32,160},{48,176},{64,192},{80,208},{96,224},{112... | collective-permute-start | bytes 30728 | tf_op jit(solution)/shard_map/ppermute | solution.py:25
  93.6 16.8 %collective-permute-start.10 = (f32[5,512]{1,0:T(8,128)S(1)}, f32[5,512]{1,0:T(8,128)S(1)}, u32[]{:S(2)}, u32[]{:S(2)}) collective-permute-start(f32[5,512]{1,0:T(8,128)S(1)} %add.109), channel_id=1, source_target_pairs={{0,256},{16,272},{32,288},{48,304},{64,320},{80,336},{96,352},{112... | collective-permute-start | bytes 30728 | tf_op jit(solution)/shard_map/ppermute | solution.py:25
  110.4 24.4 %collective-permute-start.11 = (f32[5,512]{1,0:T(8,128)S(1)}, f32[5,512]{1,0:T(8,128)S(1)}, u32[]{:S(2)}, u32[]{:S(2)}) collective-permute-start(f32[5,512]{1,0:T(8,128)S(1)} %add.110), channel_id=1, source_target_pairs={{0,512},{16,528},{32,544},{48,560},{64,576},{80,592},{96,608},{112... | collective-permute-start | bytes 30728 | tf_op jit(solution)/shard_map/ppermute | solution.py:25
  137.6 28.0 %copy-start.4 = (bf16[256,512]{1,0:T(8,128)(2,1)S(1)}, bf16[256,512]{1,0:T(8,128)(2,1)}, u32[]{:S(2)}) copy-start(bf16[256,512]{1,0:T(8,128)(2,1)} %param.11) | copy-start | bytes 786436
  137.6 27.9 %copy-start.5 = (bf16[256,512]{1,0:T(8,128)(2,1)S(1)}, bf16[256,512]{1,0:T(8,128)(2,1)}, u32[]{:S(2)}) copy-start(bf16[256,512]{1,0:T(8,128)(2,1)} %param.10) | copy-start | bytes 786436
Sparse Core Ops, SparseCore 0:
  18.3 140.7 all-gather.1

commit v2 on v1

--- a/solution.py
+++ b/solution.py
@@ -73,10 +73,9 @@
     group_w = lax.all_gather(w_out, "ylo", axis=0, tiled=True)
     group_w = lax.all_gather(group_w, "zl", axis=0, tiled=True)
     group_w = lax.all_gather(group_w, "zh", axis=0, tiled=True)
-    n_tp = out_blocks.shape[0]
-    w_blocks = group_w.reshape(group_w.shape[0], n_tp, dout.shape[1])
+    full_out = jnp.transpose(out_blocks, (1, 0, 2)).reshape(dout.shape[0], -1)
     d_gated = lax.dot_general(
-        out_blocks, w_blocks, (((0, 2), (1, 2)), ((), ())), preferred_element_type=jnp.float32
+        full_out, group_w, (((1,), (1,)), ((), ())), preferred_element_type=jnp.float32
     )
     gate_f = z_gate.astype(jnp.float32)
     grad_y = (d_gated * jax.nn.silu(gate_f)).astype(jnp.bfloat16)

time: 178 us -> 171 us (0.961)
  the two profiles are of different devices: /device:TPU:2 before, /device:TPU:4 now
where the time goes in v2:
time: 171 us; the launch traced here: 170 us
  starting transfers between devices  75.8 us (44%)
  waiting for transfers between devices  54.3 us (32%)
  between operations  14.4 us (8%)
  blocking collectives  10.9 us (6%)
  local copies, waits for them, and re-layouts  7.84 us (5%)
  matrix products  5.04 us (3%)
  other arithmetic  1.8 us (1%)
    ppermute x6, starting transfers between devices, butterfly_sum(): lax.ppermute(value, axis, [(i, i ^ 1 << b) for i in range(n)])  48.7 us
    ppermute x4, starting transfers between devices, butterfly_gather(): recv = lax.ppermute(buf, axis, [(i, i ^ 1 << b) for i in range(n)])  23.2 us
    all_gather x1, waiting for transfers between devices, local(): group_w = lax.all_gather(group_w, 'zh', axis=0, tiled=True)  22.7 us
    ppermute x6, waiting for transfers between devices, butterfly_sum(): lax.ppermute(value, axis, [(i, i ^ 1 << b) for i in range(n)])  20.3 us
    ppermute x4, waiting for transfers between devices, butterfly_gather(): recv = lax.ppermute(buf, axis, [(i, i ^ 1 << b) for i in range(n)])  11.3 us
    all_gather x1, blocking collectives, local(): group_w = lax.all_gather(group_w, 'zl', axis=0, tiled=True)  5.74 us
    all_gather x1, blocking collectives, local(): group_w = lax.all_gather(w_out, 'ylo', axis=0, tiled=True)  5.15 us
    dot_general x1, matrix products, local(): lax.dot_general(full_out, group_w, (((1,), (1,)), ((), ())), preferred_el...  5.04 us
  transfers between devices with their start and end apart: 13, of which 9 were waited for; matrix products, arithmetic and copies ran while one was open for 6% of the time, Pallas kernels for 0%

profile of v2, /device:TPU:4, one launch (start us, length us, event | category | flops | bytes accessed | tf_op | source)
XLA Modules:
  0.0 170.1 jit_solution(3357021268747460262)
XLA Ops:
  7.2 5.2 %all_gather.9 = bf16[16,4096]{1,0:T(8,128)(2,1)S(1)} all-gather(bf16[8,4096]{1,0:T(8,128)(2,1)} %param.9), channel_id=1, replica_groups=mesh['zh'=16,'zl'=2,'ylo'=2,'tp'=16] {'ylo'}, dimensions={0}, use_global_device_ids=true | all-gather | bytes 196608 | tf_op jit(solution)/shard_map/all_gather | solution.py:73
  12.4 5.7 %all_gather.10 = bf16[32,4096]{1,0:T(8,128)(2,1)} all-gather(bf16[16,4096]{1,0:T(8,128)(2,1)S(1)} %all_gather.9), channel_id=1, replica_groups=mesh['zh'=16,'zl'=2,'ylo'=2,'tp'=16] {'zl'}, dimensions={0}, use_global_device_ids=true | all-gather | bytes 393216 | tf_op jit(solution)/shard_map/all_gather | solution.py:74
  18.1 5.1 %collective-permute-start = (bf16[1,256,256]{2,1,0:T(8,128)(2,1)}, bf16[1,256,256]{2,1,0:T(8,128)(2,1)S(1)}, u32[]{:S(2)}, u32[]{:S(2)}) collective-permute-start(bf16[1,256,256]{2,1,0:T(8,128)(2,1)} %bitcast.51), channel_id=1, source_target_pairs={{0,2},{1,3},{2,0},{3,1},{4,6},{5,7},{6,4},{7,5},{8,10},{9,11},{10,... | collective-permute-start | bytes 393224 | tf_op jit(solution)/shard_map/ppermute | solution.py:34
  23.3 0.7 slice_bitcast_fusion.3
  24.0 2.6 %collective-permute-start.5 = (bf16[3,512]{1,0:T(4,128)(2,1)S(1)}, bf16[3,512]{1,0:T(4,128)(2,1)S(1)}, u32[]{:S(2)}, u32[]{:S(2)}) collective-permute-start(bf16[3,512]{1,0:T(4,128)(2,1)S(1)} %get-tuple-element.14), channel_id=1, source_target_pairs={{0,16},{16,32},{32,48},{48,64},{64,80},{80,96},{96,112},{112,128},... | collective-permute-start | bytes 9224 | tf_op jit(solution)/shard_map/ppermute | solution.py:14
  26.6 0.9 bitcast_dynamic-update-slice_fusion.7
  27.5 14.3 %collective-permute-start.1 = (bf16[2,1,256,256]{3,2,0,1:T(8,128)(2,1)S(1)}, bf16[2,1,256,256]{3,2,0,1:T(8,128)(2,1)S(1)}, u32[]{:S(2)}, u32[]{:S(2)}) collective-permute-start(bf16[2,1,256,256]{3,2,0,1:T(8,128)(2,1)S(1)} %bitcast_dynamic-update-slice_fusion.6), channel_id=1, source_target_pairs={{0,8},{1,9},{2,10},{3,11},{4,12},{5,13},{6,14},{7,15},{8,0},{9,1},... | collective-permute-start | bytes 786440 | tf_op jit(solution)/shard_map/ppermute | solution.py:34
  41.8 0.7 slice_bitcast_fusion.2
  42.6 3.6 %collective-permute-done.1 = bf16[2,1,256,256]{3,2,0,1:T(8,128)(2,1)S(1)} collective-permute-done((bf16[2,1,256,256]{3,2,0,1:T(8,128)(2,1)S(1)}, bf16[2,1,256,256]{3,2,0,1:T(8,128)(2,1)S(1)}, u32[]{:S(2)}, u32[]{:S(2)}) %collective-permute-start.1) | collective-permute-done | bytes 262176 | tf_op jit(solution)/shard_map/ppermute | solution.py:34
  46.2 1.9 %collective-permute-start.2 = (bf16[2,2,1,256,256]{4,3,1,0,2:T(8,128)(2,1)S(1)}, bf16[2,2,1,256,256]{4,3,1,0,2:T(8,128)(2,1)S(1)}, u32[]{:S(2)}, u32[]{:S(2)}) collective-permute-start(bf16[2,2,1,256,256]{4,3,1,0,2:T(8,128)(2,1)S(1)} %bitcast_dynamic-update-slice_fusion.5), channel_id=1, source_target_pairs={{0,4},{1,5},{2,6},{3,7},{4,0},{5,1},{6,2},{7,3},{8,12},{9,13},{10,... | collective-permute-start | bytes 1572872 | tf_op jit(solution)/shard_map/ppermute | solution.py:34
  48.2 1.3 collective-permute-start.4
  49.6 7.7 %collective-permute-done.2 = bf16[2,2,1,256,256]{4,3,1,0,2:T(8,128)(2,1)S(1)} collective-permute-done((bf16[2,2,1,256,256]{4,3,1,0,2:T(8,128)(2,1)S(1)}, bf16[2,2,1,256,256]{4,3,1,0,2:T(8,128)(2,1)S(1)}, u32[]{:S(2)}, u32[]{:S(2)}) %collective-permute-start.2) | collective-permute-done | bytes 524320 | tf_op jit(solution)/shard_map/ppermute | solution.py:34
  57.3 1.9 %collective-permute-start.3 = (bf16[2,2,2,1,256,256]{5,4,2,0,1,3:T(8,128)(2,1)S(1)}, bf16[2,2,2,1,256,256]{5,4,2,0,1,3:T(8,128)(2,1)}, u32[]{:S(2)}, u32[]{:S(2)}) collective-permute-start(bf16[2,2,2,1,256,256]{5,4,2,0,1,3:T(8,128)(2,1)S(1)} %bitcast_dynamic-update-slice_fusion.3), channel_id=1, source_target_pairs={{0,1},{1,0},{2,3},{3,2},{4,5},{5,4},{6,7},{7,6},{8,9},{9,8},{10,11... | collective-permute-start | bytes 3145736 | tf_op jit(solution)/shard_map/ppermute | solution.py:34
  59.9 1.2 multiply_reduce_fusion.1
  61.1 4.5 %collective-permute-start.6 = (f32[5,512]{1,0:T(8,128)S(1)}, f32[5,512]{1,0:T(8,128)S(1)}, u32[]{:S(2)}, u32[]{:S(2)}) collective-permute-start(f32[5,512]{1,0:T(8,128)S(1)} %concatenate.22), channel_id=1, source_target_pairs={{0,16},{16,0},{32,48},{48,32},{64,80},{80,64},{96,112},{112,96},{1... | collective-permute-start | bytes 30728 | tf_op jit(solution)/shard_map/ppermute | solution.py:25
  65.6 1.7 %collective-permute-done.6 = f32[5,512]{1,0:T(8,128)S(1)} collective-permute-done((f32[5,512]{1,0:T(8,128)S(1)}, f32[5,512]{1,0:T(8,128)S(1)}, u32[]{:S(2)}, u32[]{:S(2)}) %collective-permute-start.6) | collective-permute-done | bytes 10272 | tf_op jit(solution)/shard_map/ppermute | solution.py:25
  67.3 3.1 %collective-permute-start.7 = (f32[5,512]{1,0:T(8,128)S(1)}, f32[5,512]{1,0:T(8,128)S(1)}, u32[]{:S(2)}, u32[]{:S(2)}) collective-permute-start(f32[5,512]{1,0:T(8,128)S(1)} %add.106), channel_id=1, source_target_pairs={{0,32},{16,48},{32,0},{48,16},{64,96},{80,112},{96,64},{112,80},{1... | collective-permute-start | bytes 30728 | tf_op jit(solution)/shard_map/ppermute | solution.py:25
  70.5 2.9 %collective-permute-done.7 = f32[5,512]{1,0:T(8,128)S(1)} collective-permute-done((f32[5,512]{1,0:T(8,128)S(1)}, f32[5,512]{1,0:T(8,128)S(1)}, u32[]{:S(2)}, u32[]{:S(2)}) %collective-permute-start.7) | collective-permute-done | bytes 10272 | tf_op jit(solution)/shard_map/ppermute | solution.py:25
  73.3 1.9 %collective-permute-start.8 = (f32[5,512]{1,0:T(8,128)S(1)}, f32[5,512]{1,0:T(8,128)S(1)}, u32[]{:S(2)}, u32[]{:S(2)}) collective-permute-start(f32[5,512]{1,0:T(8,128)S(1)} %add.107), channel_id=1, source_target_pairs={{0,64},{16,80},{32,96},{48,112},{64,0},{80,16},{96,32},{112,48},{1... | collective-permute-start | bytes 30728 | tf_op jit(solution)/shard_map/ppermute | solution.py:25
  75.3 4.7 %collective-permute-done.8 = f32[5,512]{1,0:T(8,128)S(1)} collective-permute-done((f32[5,512]{1,0:T(8,128)S(1)}, f32[5,512]{1,0:T(8,128)S(1)}, u32[]{:S(2)}, u32[]{:S(2)}) %collective-permute-start.8) | collective-permute-done | bytes 10272 | tf_op jit(solution)/shard_map/ppermute | solution.py:25
  79.9 3.5 %collective-permute-start.9 = (f32[5,512]{1,0:T(8,128)S(1)}, f32[5,512]{1,0:T(8,128)S(1)}, u32[]{:S(2)}, u32[]{:S(2)}) collective-permute-start(f32[5,512]{1,0:T(8,128)S(1)} %add.108), channel_id=1, source_target_pairs={{0,128},{16,144},{32,160},{48,176},{64,192},{80,208},{96,224},{112... | collective-permute-start | bytes 30728 | tf_op jit(solution)/shard_map/ppermute | solution.py:25
  83.5 6.5 %collective-permute-done.9 = f32[5,512]{1,0:T(8,128)S(1)} collective-permute-done((f32[5,512]{1,0:T(8,128)S(1)}, f32[5,512]{1,0:T(8,128)S(1)}, u32[]{:S(2)}, u32[]{:S(2)}) %collective-permute-start.9) | collective-permute-done | bytes 10272 | tf_op jit(solution)/shard_map/ppermute | solution.py:25
  90.0 12.3 %collective-permute-start.10 = (f32[5,512]{1,0:T(8,128)S(1)}, f32[5,512]{1,0:T(8,128)S(1)}, u32[]{:S(2)}, u32[]{:S(2)}) collective-permute-start(f32[5,512]{1,0:T(8,128)S(1)} %add.109), channel_id=1, source_target_pairs={{0,256},{16,272},{32,288},{48,304},{64,320},{80,336},{96,352},{112... | collective-permute-start | bytes 30728 | tf_op jit(solution)/shard_map/ppermute | solution.py:25
  102.3 2.5 %collective-permute-done.10 = f32[5,512]{1,0:T(8,128)S(1)} collective-permute-done((f32[5,512]{1,0:T(8,128)S(1)}, f32[5,512]{1,0:T(8,128)S(1)}, u32[]{:S(2)}, u32[]{:S(2)}) %collective-permute-start.10) | collective-permute-done | bytes 10272 | tf_op jit(solution)/shard_map/ppermute | solution.py:25
  104.8 23.4 %collective-permute-start.11 = (f32[5,512]{1,0:T(8,128)S(1)}, f32[5,512]{1,0:T(8,128)S(1)}, u32[]{:S(2)}, u32[]{:S(2)}) collective-permute-start(f32[5,512]{1,0:T(8,128)S(1)} %add.110), channel_id=1, source_target_pairs={{0,512},{16,528},{32,544},{48,560},{64,576},{80,592},{96,608},{112... | collective-permute-start | bytes 30728 | tf_op jit(solution)/shard_map/ppermute | solution.py:25
  128.2 2.1 %collective-permute-done.11 = f32[5,512]{1,0:T(8,128)S(1)} collective-permute-done((f32[5,512]{1,0:T(8,128)S(1)}, f32[5,512]{1,0:T(8,128)S(1)}, u32[]{:S(2)}, u32[]{:S(2)}) %collective-permute-start.11) | collective-permute-done | bytes 10272 | tf_op jit(solution)/shard_map/ppermute | solution.py:25
  130.3 0.6 slice.106
  130.9 0.6 slice.107
  131.7 1.3 bitcast_dynamic-update-slice_fusion.1
  133.1 2.4 %copy.16 = bf16[256,16,256]{0,2,1:T(8,128)(2,1)} copy(bf16[256,16,256]{2,0,1:T(8,128)(2,1)S(1)} %bitcast.49) | data formatting | bytes 4194304 | tf_op jit(solution)/shard_map/transpose | solution.py:76
  135.5 22.7 %all-gather.2.cloned.1.call-done = bf16[512,4096]{1,0:T(8,128)(2,1)} async-done(((bf16[32,4096]{1,0:T(8,128)(2,1)}), bf16[512,4096]{1,0:T(8,128)(2,1)}) %all-gather.2.cloned.1.call-update) | async-done | bytes 4194320 | tf_op jit(solution)/shard_map/all_gather | solution.py:75
  158.2 5.0 %fusion.8 = (bf16[256,512]{1,0:T(8,128)(2,1)}, bf16[256,512]{1,0:T(8,128)(2,1)}) fusion(bf16[256,512]{1,0:T(8,128)(2,1)S(1)} %copy-done.4, bf16[256,512]{1,0:T(8,128)(2,1)S(1)} %copy-done.5, bf16[256,4096]{0,1:T(8,128)(2,1)} %bitcast.50, bf16[512,4096]{1,0:T(8,128)(2,1)} %all-gather.2.cloned.1.call-done), kind=kOutput, calls=%fused_computation.18 | convolution fusion | flops 1075707904 | bytes 7340032 | tf_op jit(solution)/shard_map/dot_general | solution.py:77
  (40 shorter events, 1.3 us)
Async XLA Ops:
  7.2 42.3 %copy-start.2 = (f32[4,512]{1,0:T(4,128)S(1)}, f32[4,512]{1,0:T(4,128)}, u32[]{:S(2)}) copy-start(f32[4,512]{1,0:T(4,128)} %param.14) | copy-start | bytes 24580
  7.2 151.0 %all-gather.2.cloned.1.call-start = ((), (), s32[]{:S(2)}) async-start(), calls=%async_computation | async-start | bytes 4456448 | tf_op jit(solution)/shard_map/all_gather | solution.py:75
  18.1 9.4 %collective-permute-start = (bf16[1,256,256]{2,1,0:T(8,128)(2,1)}, bf16[1,256,256]{2,1,0:T(8,128)(2,1)S(1)}, u32[]{:S(2)}, u32[]{:S(2)}) collective-permute-start(bf16[1,256,256]{2,1,0:T(8,128)(2,1)} %bitcast.51), channel_id=1, source_target_pairs={{0,2},{1,3},{2,0},{3,1},{4,6},{5,7},{6,4},{7,5},{8,10},{9,11},{10,... | collective-permute-start | bytes 393224 | tf_op jit(solution)/shard_map/ppermute | solution.py:34
  24.0 35.3 %collective-permute-start.5 = (bf16[3,512]{1,0:T(4,128)(2,1)S(1)}, bf16[3,512]{1,0:T(4,128)(2,1)S(1)}, u32[]{:S(2)}, u32[]{:S(2)}) collective-permute-start(bf16[3,512]{1,0:T(4,128)(2,1)S(1)} %get-tuple-element.14), channel_id=1, source_target_pairs={{0,16},{16,32},{32,48},{48,64},{64,80},{80,96},{96,112},{112,128},... | collective-permute-start | bytes 9224 | tf_op jit(solution)/shard_map/ppermute | solution.py:14
  27.5 18.7 %collective-permute-start.1 = (bf16[2,1,256,256]{3,2,0,1:T(8,128)(2,1)S(1)}, bf16[2,1,256,256]{3,2,0,1:T(8,128)(2,1)S(1)}, u32[]{:S(2)}, u32[]{:S(2)}) collective-permute-start(bf16[2,1,256,256]{3,2,0,1:T(8,128)(2,1)S(1)} %bitcast_dynamic-update-slice_fusion.6), channel_id=1, source_target_pairs={{0,8},{1,9},{2,10},{3,11},{4,12},{5,13},{6,14},{7,15},{8,0},{9,1},... | collective-permute-start | bytes 786440 | tf_op jit(solution)/shard_map/ppermute | solution.py:34
  42.6 16.8 %copy-start = (bf16[256,512]{1,0:T(8,128)(2,1)S(1)}, bf16[256,512]{1,0:T(8,128)(2,1)}, u32[]{:S(2)}) copy-start(bf16[256,512]{1,0:T(8,128)(2,1)} %param.12) | copy-start | bytes 786436
  42.6 16.8 %copy-start.1 = (bf16[256,512]{1,0:T(8,128)(2,1)S(1)}, bf16[256,512]{1,0:T(8,128)(2,1)}, u32[]{:S(2)}) copy-start(bf16[256,512]{1,0:T(8,128)(2,1)} %param.13) | copy-start | bytes 786436
  42.6 16.8 %copy-start.3 = (f32[512]{0:T(512)S(1)}, f32[512]{0:T(512)}, u32[]{:S(2)}) copy-start(f32[512]{0:T(512)} %param.15) | copy-start | bytes 6148
  46.2 11.1 %collective-permute-start.2 = (bf16[2,2,1,256,256]{4,3,1,0,2:T(8,128)(2,1)S(1)}, bf16[2,2,1,256,256]{4,3,1,0,2:T(8,128)(2,1)S(1)}, u32[]{:S(2)}, u32[]{:S(2)}) collective-permute-start(bf16[2,2,1,256,256]{4,3,1,0,2:T(8,128)(2,1)S(1)} %bitcast_dynamic-update-slice_fusion.5), channel_id=1, source_target_pairs={{0,4},{1,5},{2,6},{3,7},{4,0},{5,1},{6,2},{7,3},{8,12},{9,13},{10,... | collective-permute-start | bytes 1572872 | tf_op jit(solution)/shard_map/ppermute | solution.py:34
  48.2 11.1 %collective-permute-start.4 = (bf16[2,3,512]{2,1,0:T(4,128)(2,1)S(1)}, bf16[2,3,512]{2,1,0:T(4,128)(2,1)S(1)}, u32[]{:S(2)}, u32[]{:S(2)}) collective-permute-start(bf16[2,3,512]{2,1,0:T(4,128)(2,1)S(1)} %pad_maximum_fusion.2), channel_id=1, source_target_pairs={{16,0},{32,16},{48,32},{64,48},{80,64},{96,80},{112,96},{128,112},... | collective-permute-start | bytes 18440 | tf_op jit(solution)/shard_map/ppermute | solution.py:14
  57.3 74.4 %collective-permute-start.3 = (bf16[2,2,2,1,256,256]{5,4,2,0,1,3:T(8,128)(2,1)S(1)}, bf16[2,2,2,1,256,256]{5,4,2,0,1,3:T(8,128)(2,1)}, u32[]{:S(2)}, u32[]{:S(2)}) collective-permute-start(bf16[2,2,2,1,256,256]{5,4,2,0,1,3:T(8,128)(2,1)S(1)} %bitcast_dynamic-update-slice_fusion.3), channel_id=1, source_target_pairs={{0,1},{1,0},{2,3},{3,2},{4,5},{5,4},{6,7},{7,6},{8,9},{9,8},{10,11... | collective-permute-start | bytes 3145736 | tf_op jit(solution)/shard_map/ppermute | solution.py:34
  61.1 6.2 %collective-permute-start.6 = (f32[5,512]{1,0:T(8,128)S(1)}, f32[5,512]{1,0:T(8,128)S(1)}, u32[]{:S(2)}, u32[]{:S(2)}) collective-permute-start(f32[5,512]{1,0:T(8,128)S(1)} %concatenate.22), channel_id=1, source_target_pairs={{0,16},{16,0},{32,48},{48,32},{64,80},{80,64},{96,112},{112,96},{1... | collective-permute-start | bytes 30728 | tf_op jit(solution)/shard_map/ppermute | solution.py:25
  67.3 6.0 %collective-permute-start.7 = (f32[5,512]{1,0:T(8,128)S(1)}, f32[5,512]{1,0:T(8,128)S(1)}, u32[]{:S(2)}, u32[]{:S(2)}) collective-permute-start(f32[5,512]{1,0:T(8,128)S(1)} %add.106), channel_id=1, source_target_pairs={{0,32},{16,48},{32,0},{48,16},{64,96},{80,112},{96,64},{112,80},{1... | collective-permute-start | bytes 30728 | tf_op jit(solution)/shard_map/ppermute | solution.py:25
  73.3 6.6 %collective-permute-start.8 = (f32[5,512]{1,0:T(8,128)S(1)}, f32[5,512]{1,0:T(8,128)S(1)}, u32[]{:S(2)}, u32[]{:S(2)}) collective-permute-start(f32[5,512]{1,0:T(8,128)S(1)} %add.107), channel_id=1, source_target_pairs={{0,64},{16,80},{32,96},{48,112},{64,0},{80,16},{96,32},{112,48},{1... | collective-permute-start | bytes 30728 | tf_op jit(solution)/shard_map/ppermute | solution.py:25
  79.9 10.1 %collective-permute-start.9 = (f32[5,512]{1,0:T(8,128)S(1)}, f32[5,512]{1,0:T(8,128)S(1)}, u32[]{:S(2)}, u32[]{:S(2)}) collective-permute-start(f32[5,512]{1,0:T(8,128)S(1)} %add.108), channel_id=1, source_target_pairs={{0,128},{16,144},{32,160},{48,176},{64,192},{80,208},{96,224},{112... | collective-permute-start | bytes 30728 | tf_op jit(solution)/shard_map/ppermute | solution.py:25
  90.0 14.8 %collective-permute-start.10 = (f32[5,512]{1,0:T(8,128)S(1)}, f32[5,512]{1,0:T(8,128)S(1)}, u32[]{:S(2)}, u32[]{:S(2)}) collective-permute-start(f32[5,512]{1,0:T(8,128)S(1)} %add.109), channel_id=1, source_target_pairs={{0,256},{16,272},{32,288},{48,304},{64,320},{80,336},{96,352},{112... | collective-permute-start | bytes 30728 | tf_op jit(solution)/shard_map/ppermute | solution.py:25
  104.8 25.5 %collective-permute-start.11 = (f32[5,512]{1,0:T(8,128)S(1)}, f32[5,512]{1,0:T(8,128)S(1)}, u32[]{:S(2)}, u32[]{:S(2)}) collective-permute-start(f32[5,512]{1,0:T(8,128)S(1)} %add.110), channel_id=1, source_target_pairs={{0,512},{16,528},{32,544},{48,560},{64,576},{80,592},{96,608},{112... | collective-permute-start | bytes 30728 | tf_op jit(solution)/shard_map/ppermute | solution.py:25
  133.1 25.1 %copy-start.4 = (bf16[256,512]{1,0:T(8,128)(2,1)S(1)}, bf16[256,512]{1,0:T(8,128)(2,1)}, u32[]{:S(2)}) copy-start(bf16[256,512]{1,0:T(8,128)(2,1)} %param.11) | copy-start | bytes 786436
  133.1 25.1 %copy-start.5 = (bf16[256,512]{1,0:T(8,128)(2,1)S(1)}, bf16[256,512]{1,0:T(8,128)(2,1)}, u32[]{:S(2)}) copy-start(bf16[256,512]{1,0:T(8,128)(2,1)} %param.10) | copy-start | bytes 786436
Sparse Core Ops, SparseCore 0:
  18.3 139.8 all-gather.1

commit v3 on v2

--- a/solution.py
+++ b/solution.py
@@ -68,6 +68,10 @@
     fsdp_bits = (lax.axis_size(FSDP) - 1).bit_length()
     total = butterfly_sum(partial, FSDP, list(range(fsdp_bits)))
     grad_w, grad_b = total[:KW], total[KW]
+    gate_f = z_gate.astype(jnp.float32)
+    y_factor = jax.nn.silu(gate_f)
+    z_factor = y_scan.astype(jnp.float32) * silu_slope(gate_f)
+    y_factor, z_factor = lax.optimization_barrier((y_factor, z_factor))
     tp_bits = (lax.axis_size("tp") - 1).bit_length()
     out_blocks = butterfly_gather(dout, "tp", [1] + list(range(tp_bits - 1, 1, -1)) + [0])
     group_w = lax.all_gather(w_out, "ylo", axis=0, tiled=True)
@@ -77,9 +81,8 @@
     d_gated = lax.dot_general(
         full_out, group_w, (((1,), (1,)), ((), ())), preferred_element_type=jnp.float32
     )
-    gate_f = z_gate.astype(jnp.float32)
-    grad_y = (d_gated * jax.nn.silu(gate_f)).astype(jnp.bfloat16)
-    grad_z = (d_gated * y_scan.astype(jnp.float32) * silu_slope(gate_f)).astype(jnp.bfloat16)
+    grad_y = (d_gated * y_factor).astype(jnp.bfloat16)
+    grad_z = (d_gated * z_factor).astype(jnp.bfloat16)
     return (grad_y, grad_z, grad_x.astype(jnp.bfloat16), grad_w, grad_b)
 
 

time: 171 us -> 172 us (level)
  the two profiles are of different devices: /device:TPU:4 before, /device:TPU:20 now
where the time goes in v3:
time: 172 us; the launch traced here: 171 us
  starting transfers between devices  72.3 us (42%)
  waiting for transfers between devices  56.6 us (33%)
  between operations  14.4 us (8%)
  blocking collectives  11 us (6%)
  local copies, waits for them, and re-layouts  8.72 us (5%)
  matrix products  4.91 us (3%)
  other arithmetic  3.04 us (2%)
    ppermute x6, starting transfers between devices, butterfly_sum(): lax.ppermute(value, axis, [(i, i ^ 1 << b) for i in range(n)])  46.6 us
    ppermute x6, waiting for transfers between devices, butterfly_sum(): lax.ppermute(value, axis, [(i, i ^ 1 << b) for i in range(n)])  24.1 us
    ppermute x4, starting transfers between devices, butterfly_gather(): recv = lax.ppermute(buf, axis, [(i, i ^ 1 << b) for i in range(n)])  20.3 us
    all_gather x1, waiting for transfers between devices, local(): group_w = lax.all_gather(group_w, 'zh', axis=0, tiled=True)  20.1 us
    ppermute x4, waiting for transfers between devices, butterfly_gather(): recv = lax.ppermute(buf, axis, [(i, i ^ 1 << b) for i in range(n)])  12.4 us
    all_gather x1, blocking collectives, local(): group_w = lax.all_gather(group_w, 'zl', axis=0, tiled=True)  5.74 us
    ppermute x2, starting transfers between devices, shifted(): return lax.ppermute(block, axis, route)  5.37 us
    all_gather x1, blocking collectives, local(): group_w = lax.all_gather(w_out, 'ylo', axis=0, tiled=True)  5.29 us
  transfers between devices with their start and end apart: 13, of which 9 were waited for; matrix products, arithmetic and copies ran while one was open for 7% of the time, Pallas kernels for 0%

profile of v3, /device:TPU:20, one launch (start us, length us, event | category | flops | bytes accessed | tf_op | source)
XLA Modules:
  0.0 171.0 jit_solution(13840034450069316805)
XLA Ops:
  7.2 5.3 %all_gather.9 = bf16[16,4096]{1,0:T(8,128)(2,1)S(1)} all-gather(bf16[8,4096]{1,0:T(8,128)(2,1)} %param.9), channel_id=1, replica_groups=mesh['zh'=16,'zl'=2,'ylo'=2,'tp'=16] {'ylo'}, dimensions={0}, use_global_device_ids=true | all-gather | bytes 196608 | tf_op jit(solution)/shard_map/all_gather | solution.py:77
  12.5 5.7 %all_gather.10 = bf16[32,4096]{1,0:T(8,128)(2,1)} all-gather(bf16[16,4096]{1,0:T(8,128)(2,1)S(1)} %all_gather.9), channel_id=1, replica_groups=mesh['zh'=16,'zl'=2,'ylo'=2,'tp'=16] {'zl'}, dimensions={0}, use_global_device_ids=true | all-gather | bytes 393216 | tf_op jit(solution)/shard_map/all_gather | solution.py:78
  18.3 2.2 %collective-permute-start = (bf16[1,256,256]{2,1,0:T(8,128)(2,1)}, bf16[1,256,256]{2,1,0:T(8,128)(2,1)S(1)}, u32[]{:S(2)}, u32[]{:S(2)}) collective-permute-start(bf16[1,256,256]{2,1,0:T(8,128)(2,1)} %bitcast.51), channel_id=1, source_target_pairs={{0,2},{1,3},{2,0},{3,1},{4,6},{5,7},{6,4},{7,5},{8,10},{9,11},{10,... | collective-permute-start | bytes 393224 | tf_op jit(solution)/shard_map/ppermute | solution.py:34
  20.5 0.7 slice_bitcast_fusion.3
  21.3 4.1 %collective-permute-start.5 = (bf16[3,512]{1,0:T(4,128)(2,1)S(1)}, bf16[3,512]{1,0:T(4,128)(2,1)S(1)}, u32[]{:S(2)}, u32[]{:S(2)}) collective-permute-start(bf16[3,512]{1,0:T(4,128)(2,1)S(1)} %get-tuple-element.18), channel_id=1, source_target_pairs={{0,16},{16,32},{32,48},{48,64},{64,80},{80,96},{96,112},{112,128},... | collective-permute-start | bytes 9224 | tf_op jit(solution)/shard_map/ppermute | solution.py:14
  25.3 0.7 slice_bitcast_fusion.2
  26.1 1.3 collective-permute-start.4
  27.4 0.9 bitcast_dynamic-update-slice_fusion.7
  28.3 14.2 %collective-permute-start.1 = (bf16[2,1,256,256]{3,2,0,1:T(8,128)(2,1)S(1)}, bf16[2,1,256,256]{3,2,0,1:T(8,128)(2,1)S(1)}, u32[]{:S(2)}, u32[]{:S(2)}) collective-permute-start(bf16[2,1,256,256]{3,2,0,1:T(8,128)(2,1)S(1)} %bitcast_dynamic-update-slice_fusion.6), channel_id=1, source_target_pairs={{0,8},{1,9},{2,10},{3,11},{4,12},{5,13},{6,14},{7,15},{8,0},{9,1},... | collective-permute-start | bytes 786440 | tf_op jit(solution)/shard_map/ppermute | solution.py:34
  42.5 0.9 fusion.13
  43.5 3.5 %collective-permute-done.1 = bf16[2,1,256,256]{3,2,0,1:T(8,128)(2,1)S(1)} collective-permute-done((bf16[2,1,256,256]{3,2,0,1:T(8,128)(2,1)S(1)}, bf16[2,1,256,256]{3,2,0,1:T(8,128)(2,1)S(1)}, u32[]{:S(2)}, u32[]{:S(2)}) %collective-permute-start.1) | collective-permute-done | bytes 262176 | tf_op jit(solution)/shard_map/ppermute | solution.py:34
  47.0 1.9 %collective-permute-start.2 = (bf16[2,2,1,256,256]{4,3,1,0,2:T(8,128)(2,1)S(1)}, bf16[2,2,1,256,256]{4,3,1,0,2:T(8,128)(2,1)S(1)}, u32[]{:S(2)}, u32[]{:S(2)}) collective-permute-start(bf16[2,2,1,256,256]{4,3,1,0,2:T(8,128)(2,1)S(1)} %bitcast_dynamic-update-slice_fusion.5), channel_id=1, source_target_pairs={{0,4},{1,5},{2,6},{3,7},{4,0},{5,1},{6,2},{7,3},{8,12},{9,13},{10,... | collective-permute-start | bytes 1572872 | tf_op jit(solution)/shard_map/ppermute | solution.py:34
  49.2 8.9 %collective-permute-done.2 = bf16[2,2,1,256,256]{4,3,1,0,2:T(8,128)(2,1)S(1)} collective-permute-done((bf16[2,2,1,256,256]{4,3,1,0,2:T(8,128)(2,1)S(1)}, bf16[2,2,1,256,256]{4,3,1,0,2:T(8,128)(2,1)S(1)}, u32[]{:S(2)}, u32[]{:S(2)}) %collective-permute-start.2) | collective-permute-done | bytes 524320 | tf_op jit(solution)/shard_map/ppermute | solution.py:34
  58.1 1.9 %collective-permute-start.3 = (bf16[2,2,2,1,256,256]{5,4,2,0,1,3:T(8,128)(2,1)S(1)}, bf16[2,2,2,1,256,256]{5,4,2,0,1,3:T(8,128)(2,1)}, u32[]{:S(2)}, u32[]{:S(2)}) collective-permute-start(bf16[2,2,2,1,256,256]{5,4,2,0,1,3:T(8,128)(2,1)S(1)} %bitcast_dynamic-update-slice_fusion.3), channel_id=1, source_target_pairs={{0,1},{1,0},{2,3},{3,2},{4,5},{5,4},{6,7},{7,6},{8,9},{9,8},{10,11... | collective-permute-start | bytes 3145736 | tf_op jit(solution)/shard_map/ppermute | solution.py:34
  60.6 1.2 multiply_reduce_fusion.1
  61.8 4.4 %collective-permute-start.6 = (f32[5,512]{1,0:T(8,128)S(1)}, f32[5,512]{1,0:T(8,128)S(1)}, u32[]{:S(2)}, u32[]{:S(2)}) collective-permute-start(f32[5,512]{1,0:T(8,128)S(1)} %concatenate.22), channel_id=1, source_target_pairs={{0,16},{16,0},{32,48},{48,32},{64,80},{80,64},{96,112},{112,96},{1... | collective-permute-start | bytes 30728 | tf_op jit(solution)/shard_map/ppermute | solution.py:25
  66.3 1.7 collective-permute-done.6
  68.0 4.2 %collective-permute-start.7 = (f32[5,512]{1,0:T(8,128)S(1)}, f32[5,512]{1,0:T(8,128)S(1)}, u32[]{:S(2)}, u32[]{:S(2)}) collective-permute-start(f32[5,512]{1,0:T(8,128)S(1)} %add.106), channel_id=1, source_target_pairs={{0,32},{16,48},{32,0},{48,16},{64,96},{80,112},{96,64},{112,80},{1... | collective-permute-start | bytes 30728 | tf_op jit(solution)/shard_map/ppermute | solution.py:25
  72.2 2.4 %collective-permute-done.7 = f32[5,512]{1,0:T(8,128)S(1)} collective-permute-done((f32[5,512]{1,0:T(8,128)S(1)}, f32[5,512]{1,0:T(8,128)S(1)}, u32[]{:S(2)}, u32[]{:S(2)}) %collective-permute-start.7) | collective-permute-done | bytes 10272 | tf_op jit(solution)/shard_map/ppermute | solution.py:25
  74.7 5.2 %collective-permute-start.8 = (f32[5,512]{1,0:T(8,128)S(1)}, f32[5,512]{1,0:T(8,128)S(1)}, u32[]{:S(2)}, u32[]{:S(2)}) collective-permute-start(f32[5,512]{1,0:T(8,128)S(1)} %add.107), channel_id=1, source_target_pairs={{0,64},{16,80},{32,96},{48,112},{64,0},{80,16},{96,32},{112,48},{1... | collective-permute-start | bytes 30728 | tf_op jit(solution)/shard_map/ppermute | solution.py:25
  79.9 4.1 %collective-permute-done.8 = f32[5,512]{1,0:T(8,128)S(1)} collective-permute-done((f32[5,512]{1,0:T(8,128)S(1)}, f32[5,512]{1,0:T(8,128)S(1)}, u32[]{:S(2)}, u32[]{:S(2)}) %collective-permute-start.8) | collective-permute-done | bytes 10272 | tf_op jit(solution)/shard_map/ppermute | solution.py:25
  84.0 1.9 %collective-permute-start.9 = (f32[5,512]{1,0:T(8,128)S(1)}, f32[5,512]{1,0:T(8,128)S(1)}, u32[]{:S(2)}, u32[]{:S(2)}) collective-permute-start(f32[5,512]{1,0:T(8,128)S(1)} %add.108), channel_id=1, source_target_pairs={{0,128},{16,144},{32,160},{48,176},{64,192},{80,208},{96,224},{112... | collective-permute-start | bytes 30728 | tf_op jit(solution)/shard_map/ppermute | solution.py:25
  85.9 8.6 %collective-permute-done.9 = f32[5,512]{1,0:T(8,128)S(1)} collective-permute-done((f32[5,512]{1,0:T(8,128)S(1)}, f32[5,512]{1,0:T(8,128)S(1)}, u32[]{:S(2)}, u32[]{:S(2)}) %collective-permute-start.9) | collective-permute-done | bytes 10272 | tf_op jit(solution)/shard_map/ppermute | solution.py:25
  94.5 8.7 %collective-permute-start.10 = (f32[5,512]{1,0:T(8,128)S(1)}, f32[5,512]{1,0:T(8,128)S(1)}, u32[]{:S(2)}, u32[]{:S(2)}) collective-permute-start(f32[5,512]{1,0:T(8,128)S(1)} %add.109), channel_id=1, source_target_pairs={{0,256},{16,272},{32,288},{48,304},{64,320},{80,336},{96,352},{112... | collective-permute-start | bytes 30728 | tf_op jit(solution)/shard_map/ppermute | solution.py:25
  103.1 6.4 %collective-permute-done.10 = f32[5,512]{1,0:T(8,128)S(1)} collective-permute-done((f32[5,512]{1,0:T(8,128)S(1)}, f32[5,512]{1,0:T(8,128)S(1)}, u32[]{:S(2)}, u32[]{:S(2)}) %collective-permute-start.10) | collective-permute-done | bytes 10272 | tf_op jit(solution)/shard_map/ppermute | solution.py:25
  109.5 22.2 %collective-permute-start.11 = (f32[5,512]{1,0:T(8,128)S(1)}, f32[5,512]{1,0:T(8,128)S(1)}, u32[]{:S(2)}, u32[]{:S(2)}) collective-permute-start(f32[5,512]{1,0:T(8,128)S(1)} %add.110), channel_id=1, source_target_pairs={{0,512},{16,528},{32,544},{48,560},{64,576},{80,592},{96,608},{112... | collective-permute-start | bytes 30728 | tf_op jit(solution)/shard_map/ppermute | solution.py:25
  131.8 1.2 fusion.5
  133.0 0.9 collective-permute-done.11
  135.4 1.3 bitcast_dynamic-update-slice_fusion.1
  136.8 2.4 %copy.16 = bf16[256,16,256]{0,2,1:T(8,128)(2,1)} copy(bf16[256,16,256]{2,0,1:T(8,128)(2,1)S(1)} %bitcast.49) | data formatting | bytes 4194304 | tf_op jit(solution)/shard_map/transpose | solution.py:80
  139.1 20.1 %all-gather.2.cloned.1.call-done = bf16[512,4096]{1,0:T(8,128)(2,1)} async-done(((bf16[32,4096]{1,0:T(8,128)(2,1)}), bf16[512,4096]{1,0:T(8,128)(2,1)}) %all-gather.2.cloned.1.call-update) | async-done | bytes 4194320 | tf_op jit(solution)/shard_map/all_gather | solution.py:79
  159.2 4.9 %multiply_convert_fusion = (bf16[256,512]{1,0:T(8,128)(2,1)}, bf16[256,512]{1,0:T(8,128)(2,1)}) fusion(f32[256,512]{1,0:T(8,128)S(1)} %copy-done.1, f32[256,512]{1,0:T(8,128)S(1)} %copy-done.2, bf16[256,4096]{0,1:T(8,128)(2,1)} %bitcast.50, bf16[512,4096]{1,0:T(8,128)(2,1)} %all-gather.2.cloned.1.call-done), kind=kOutput, calls=%fused_computation.29 | convolution fusion | flops 1074266112 | bytes 7864320 | tf_op jit(solution)/shard_map/dot_general | solution.py:81
  (43 shorter events, 2.5 us)
Async XLA Ops:
  7.2 41.8 %copy-start = (bf16[256,512]{1,0:T(8,128)(2,1)S(1)}, bf16[256,512]{1,0:T(8,128)(2,1)}, u32[]{:S(2)}) copy-start(bf16[256,512]{1,0:T(8,128)(2,1)} %param.12) | copy-start | bytes 786436
  7.2 152.1 %all-gather.2.cloned.1.call-start = ((), (), s32[]{:S(2)}) async-start(), calls=%async_computation | async-start | bytes 4456448 | tf_op jit(solution)/shard_map/all_gather | solution.py:79
  18.3 10.0 %collective-permute-start = (bf16[1,256,256]{2,1,0:T(8,128)(2,1)}, bf16[1,256,256]{2,1,0:T(8,128)(2,1)S(1)}, u32[]{:S(2)}, u32[]{:S(2)}) collective-permute-start(bf16[1,256,256]{2,1,0:T(8,128)(2,1)} %bitcast.51), channel_id=1, source_target_pairs={{0,2},{1,3},{2,0},{3,1},{4,6},{5,7},{6,4},{7,5},{8,10},{9,11},{10,... | collective-permute-start | bytes 393224 | tf_op jit(solution)/shard_map/ppermute | solution.py:34
  21.3 27.7 %collective-permute-start.5 = (bf16[3,512]{1,0:T(4,128)(2,1)S(1)}, bf16[3,512]{1,0:T(4,128)(2,1)S(1)}, u32[]{:S(2)}, u32[]{:S(2)}) collective-permute-start(bf16[3,512]{1,0:T(4,128)(2,1)S(1)} %get-tuple-element.18), channel_id=1, source_target_pairs={{0,16},{16,32},{32,48},{48,64},{64,80},{80,96},{96,112},{112,128},... | collective-permute-start | bytes 9224 | tf_op jit(solution)/shard_map/ppermute | solution.py:14
  26.1 22.9 %collective-permute-start.4 = (bf16[2,3,512]{2,1,0:T(4,128)(2,1)S(1)}, bf16[2,3,512]{2,1,0:T(4,128)(2,1)S(1)}, u32[]{:S(2)}, u32[]{:S(2)}) collective-permute-start(bf16[2,3,512]{2,1,0:T(4,128)(2,1)S(1)} %pad_maximum_fusion.2), channel_id=1, source_target_pairs={{16,0},{32,16},{48,32},{64,48},{80,64},{96,80},{112,96},{128,112},... | collective-permute-start | bytes 18440 | tf_op jit(solution)/shard_map/ppermute | solution.py:14
  28.3 18.7 %collective-permute-start.1 = (bf16[2,1,256,256]{3,2,0,1:T(8,128)(2,1)S(1)}, bf16[2,1,256,256]{3,2,0,1:T(8,128)(2,1)S(1)}, u32[]{:S(2)}, u32[]{:S(2)}) collective-permute-start(bf16[2,1,256,256]{3,2,0,1:T(8,128)(2,1)S(1)} %bitcast_dynamic-update-slice_fusion.6), channel_id=1, source_target_pairs={{0,8},{1,9},{2,10},{3,11},{4,12},{5,13},{6,14},{7,15},{8,0},{9,1},... | collective-permute-start | bytes 786440 | tf_op jit(solution)/shard_map/ppermute | solution.py:34
  43.5 16.6 %copy-start.3 = (bf16[256,512]{1,0:T(8,128)(2,1)S(1)}, bf16[256,512]{1,0:T(8,128)(2,1)}, u32[]{:S(2)}) copy-start(bf16[256,512]{1,0:T(8,128)(2,1)} %param.13) | copy-start | bytes 786436
  43.5 16.6 %copy-start.6 = (f32[512]{0:T(512)S(1)}, f32[512]{0:T(512)}, u32[]{:S(2)}) copy-start(f32[512]{0:T(512)} %param.15) | copy-start | bytes 6148
  47.0 11.1 %collective-permute-start.2 = (bf16[2,2,1,256,256]{4,3,1,0,2:T(8,128)(2,1)S(1)}, bf16[2,2,1,256,256]{4,3,1,0,2:T(8,128)(2,1)S(1)}, u32[]{:S(2)}, u32[]{:S(2)}) collective-permute-start(bf16[2,2,1,256,256]{4,3,1,0,2:T(8,128)(2,1)S(1)} %bitcast_dynamic-update-slice_fusion.5), channel_id=1, source_target_pairs={{0,4},{1,5},{2,6},{3,7},{4,0},{5,1},{6,2},{7,3},{8,12},{9,13},{10,... | collective-permute-start | bytes 1572872 | tf_op jit(solution)/shard_map/ppermute | solution.py:34
  58.1 77.3 %collective-permute-start.3 = (bf16[2,2,2,1,256,256]{5,4,2,0,1,3:T(8,128)(2,1)S(1)}, bf16[2,2,2,1,256,256]{5,4,2,0,1,3:T(8,128)(2,1)}, u32[]{:S(2)}, u32[]{:S(2)}) collective-permute-start(bf16[2,2,2,1,256,256]{5,4,2,0,1,3:T(8,128)(2,1)S(1)} %bitcast_dynamic-update-slice_fusion.3), channel_id=1, source_target_pairs={{0,1},{1,0},{2,3},{3,2},{4,5},{5,4},{6,7},{7,6},{8,9},{9,8},{10,11... | collective-permute-start | bytes 3145736 | tf_op jit(solution)/shard_map/ppermute | solution.py:34
  60.1 71.7 %copy-start.4 = (bf16[256,512]{1,0:T(8,128)(2,1)S(1)}, bf16[256,512]{1,0:T(8,128)(2,1)}, u32[]{:S(2)}) copy-start(bf16[256,512]{1,0:T(8,128)(2,1)} %param.11) | copy-start | bytes 786436
  60.1 71.7 %copy-start.5 = (bf16[256,512]{1,0:T(8,128)(2,1)S(1)}, bf16[256,512]{1,0:T(8,128)(2,1)}, u32[]{:S(2)}) copy-start(bf16[256,512]{1,0:T(8,128)(2,1)} %param.10) | copy-start | bytes 786436
  61.8 6.1 %collective-permute-start.6 = (f32[5,512]{1,0:T(8,128)S(1)}, f32[5,512]{1,0:T(8,128)S(1)}, u32[]{:S(2)}, u32[]{:S(2)}) collective-permute-start(f32[5,512]{1,0:T(8,128)S(1)} %concatenate.22), channel_id=1, source_target_pairs={{0,16},{16,0},{32,48},{48,32},{64,80},{80,64},{96,112},{112,96},{1... | collective-permute-start | bytes 30728 | tf_op jit(solution)/shard_map/ppermute | solution.py:25
  68.0 6.7 %collective-permute-start.7 = (f32[5,512]{1,0:T(8,128)S(1)}, f32[5,512]{1,0:T(8,128)S(1)}, u32[]{:S(2)}, u32[]{:S(2)}) collective-permute-start(f32[5,512]{1,0:T(8,128)S(1)} %add.106), channel_id=1, source_target_pairs={{0,32},{16,48},{32,0},{48,16},{64,96},{80,112},{96,64},{112,80},{1... | collective-permute-start | bytes 30728 | tf_op jit(solution)/shard_map/ppermute | solution.py:25
  74.7 9.3 %collective-permute-start.8 = (f32[5,512]{1,0:T(8,128)S(1)}, f32[5,512]{1,0:T(8,128)S(1)}, u32[]{:S(2)}, u32[]{:S(2)}) collective-permute-start(f32[5,512]{1,0:T(8,128)S(1)} %add.107), channel_id=1, source_target_pairs={{0,64},{16,80},{32,96},{48,112},{64,0},{80,16},{96,32},{112,48},{1... | collective-permute-start | bytes 30728 | tf_op jit(solution)/shard_map/ppermute | solution.py:25
  84.0 10.5 %collective-permute-start.9 = (f32[5,512]{1,0:T(8,128)S(1)}, f32[5,512]{1,0:T(8,128)S(1)}, u32[]{:S(2)}, u32[]{:S(2)}) collective-permute-start(f32[5,512]{1,0:T(8,128)S(1)} %add.108), channel_id=1, source_target_pairs={{0,128},{16,144},{32,160},{48,176},{64,192},{80,208},{96,224},{112... | collective-permute-start | bytes 30728 | tf_op jit(solution)/shard_map/ppermute | solution.py:25
  94.5 15.1 %collective-permute-start.10 = (f32[5,512]{1,0:T(8,128)S(1)}, f32[5,512]{1,0:T(8,128)S(1)}, u32[]{:S(2)}, u32[]{:S(2)}) collective-permute-start(f32[5,512]{1,0:T(8,128)S(1)} %add.109), channel_id=1, source_target_pairs={{0,256},{16,272},{32,288},{48,304},{64,320},{80,336},{96,352},{112... | collective-permute-start | bytes 30728 | tf_op jit(solution)/shard_map/ppermute | solution.py:25
  109.5 24.4 %collective-permute-start.11 = (f32[5,512]{1,0:T(8,128)S(1)}, f32[5,512]{1,0:T(8,128)S(1)}, u32[]{:S(2)}, u32[]{:S(2)}) collective-permute-start(f32[5,512]{1,0:T(8,128)S(1)} %add.110), channel_id=1, source_target_pairs={{0,512},{16,528},{32,544},{48,560},{64,576},{80,592},{96,608},{112... | collective-permute-start | bytes 30728 | tf_op jit(solution)/shard_map/ppermute | solution.py:25
  136.7 22.5 %copy-start.1 = (f32[256,512]{1,0:T(8,128)S(1)}, f32[256,512]{1,0:T(8,128)}, u32[]{:S(2)}) copy-start(f32[256,512]{1,0:T(8,128)} %get-tuple-element.8) | copy-start | bytes 1572868
  136.7 22.5 %copy-start.2 = (f32[256,512]{1,0:T(8,128)S(1)}, f32[256,512]{1,0:T(8,128)}, u32[]{:S(2)}) copy-start(f32[256,512]{1,0:T(8,128)} %get-tuple-element.7) | copy-start | bytes 1572868
Sparse Core Ops, SparseCore 0:
  18.4 140.7 all-gather.1

commit v4 on v2

--- a/solution.py
+++ b/solution.py
@@ -70,8 +70,7 @@
     grad_w, grad_b = total[:KW], total[KW]
     tp_bits = (lax.axis_size("tp") - 1).bit_length()
     out_blocks = butterfly_gather(dout, "tp", [1] + list(range(tp_bits - 1, 1, -1)) + [0])
-    group_w = lax.all_gather(w_out, "ylo", axis=0, tiled=True)
-    group_w = lax.all_gather(group_w, "zl", axis=0, tiled=True)
+    group_w = lax.all_gather(w_out, ("zl", "ylo"), axis=0, tiled=True)
     group_w = lax.all_gather(group_w, "zh", axis=0, tiled=True)
     full_out = jnp.transpose(out_blocks, (1, 0, 2)).reshape(dout.shape[0], -1)
     d_gated = lax.dot_general(

time: 171 us -> 174 us (1.018)
  the two profiles are of different devices: /device:TPU:4 before, /device:TPU:30 now
where the time goes in v4:
time: 174 us
  starting transfers between devices  72.4 us (42%)
  waiting for transfers between devices  58.8 us (34%)
  between operations  14.4 us (8%)
  blocking collectives  13.4 us (8%)
  local copies, waits for them, and re-layouts  7.83 us (4%)
  matrix products  5.04 us (3%)
  other arithmetic  1.8 us (1%)
    ppermute x6, starting transfers between devices, butterfly_sum(): lax.ppermute(value, axis, [(i, i ^ 1 << b) for i in range(n)])  47.6 us
    all_gather x1, waiting for transfers between devices, local(): group_w = lax.all_gather(group_w, 'zh', axis=0, tiled=True)  25.2 us
    ppermute x6, waiting for transfers between devices, butterfly_sum(): lax.ppermute(value, axis, [(i, i ^ 1 << b) for i in range(n)])  23.2 us
    ppermute x4, starting transfers between devices, butterfly_gather(): recv = lax.ppermute(buf, axis, [(i, i ^ 1 << b) for i in range(n)])  18.8 us
    all_gather x1, blocking collectives, local(): group_w = lax.all_gather(w_out, ('zl', 'ylo'), axis=0, tiled=True)  13.4 us
    ppermute x4, waiting for transfers between devices, butterfly_gather(): recv = lax.ppermute(buf, axis, [(i, i ^ 1 << b) for i in range(n)])  10.4 us
    ppermute x2, starting transfers between devices, shifted(): return lax.ppermute(block, axis, route)  5.94 us
    dot_general x1, matrix products, local(): lax.dot_general(full_out, group_w, (((1,), (1,)), ((), ())), preferred_el...  5.04 us
  transfers between devices with their start and end apart: 13, of which 10 were waited for; matrix products, arithmetic and copies ran while one was open for 6% of the time, Pallas kernels for 0%

profile of v4, /device:TPU:30, one launch (start us, length us, event | category | flops | bytes accessed | tf_op | source)
XLA Modules:
  0.0 173.7 jit_solution(2902269950622423594)
XLA Ops:
  7.2 13.4 %all_gather.6 = bf16[32,4096]{1,0:T(8,128)(2,1)} all-gather(bf16[8,4096]{1,0:T(8,128)(2,1)} %param.9), channel_id=1, replica_groups=mesh['zh'=16,'zl'=2,'ylo'=2,'tp'=16] {'zl','ylo'}, dimensions={0}, use_global_device_ids=true | all-gather | bytes 327680 | tf_op jit(solution)/shard_map/all_gather | solution.py:73
  20.6 3.1 %collective-permute-start = (bf16[1,256,256]{2,1,0:T(8,128)(2,1)}, bf16[1,256,256]{2,1,0:T(8,128)(2,1)S(1)}, u32[]{:S(2)}, u32[]{:S(2)}) collective-permute-start(bf16[1,256,256]{2,1,0:T(8,128)(2,1)} %bitcast.51), channel_id=1, source_target_pairs={{0,2},{1,3},{2,0},{3,1},{4,6},{5,7},{6,4},{7,5},{8,10},{9,11},{10,... | collective-permute-start | bytes 393224 | tf_op jit(solution)/shard_map/ppermute | solution.py:34
  23.8 0.7 slice_bitcast_fusion.3
  24.5 2.8 %collective-permute-start.5 = (bf16[3,512]{1,0:T(4,128)(2,1)S(1)}, bf16[3,512]{1,0:T(4,128)(2,1)S(1)}, u32[]{:S(2)}, u32[]{:S(2)}) collective-permute-start(bf16[3,512]{1,0:T(4,128)(2,1)S(1)} %get-tuple-element.14), channel_id=1, source_target_pairs={{0,16},{16,32},{32,48},{48,64},{64,80},{80,96},{96,112},{112,128},... | collective-permute-start | bytes 9224 | tf_op jit(solution)/shard_map/ppermute | solution.py:14
  27.3 0.9 bitcast_dynamic-update-slice_fusion.7
  28.3 0.9 collective-permute-done
  29.2 3.3 %collective-permute-start.1 = (bf16[2,1,256,256]{3,2,0,1:T(8,128)(2,1)S(1)}, bf16[2,1,256,256]{3,2,0,1:T(8,128)(2,1)S(1)}, u32[]{:S(2)}, u32[]{:S(2)}) collective-permute-start(bf16[2,1,256,256]{3,2,0,1:T(8,128)(2,1)S(1)} %bitcast_dynamic-update-slice_fusion.6), channel_id=1, source_target_pairs={{0,8},{1,9},{2,10},{3,11},{4,12},{5,13},{6,14},{7,15},{8,0},{9,1},... | collective-permute-start | bytes 786440 | tf_op jit(solution)/shard_map/ppermute | solution.py:34
  32.6 0.7 slice_bitcast_fusion.2
  33.4 5.6 %collective-permute-done.1 = bf16[2,1,256,256]{3,2,0,1:T(8,128)(2,1)S(1)} collective-permute-done((bf16[2,1,256,256]{3,2,0,1:T(8,128)(2,1)S(1)}, bf16[2,1,256,256]{3,2,0,1:T(8,128)(2,1)S(1)}, u32[]{:S(2)}, u32[]{:S(2)}) %collective-permute-start.1) | collective-permute-done | bytes 262176 | tf_op jit(solution)/shard_map/ppermute | solution.py:34
  39.0 10.5 %collective-permute-start.2 = (bf16[2,2,1,256,256]{4,3,1,0,2:T(8,128)(2,1)S(1)}, bf16[2,2,1,256,256]{4,3,1,0,2:T(8,128)(2,1)S(1)}, u32[]{:S(2)}, u32[]{:S(2)}) collective-permute-start(bf16[2,2,1,256,256]{4,3,1,0,2:T(8,128)(2,1)S(1)} %bitcast_dynamic-update-slice_fusion.5), channel_id=1, source_target_pairs={{0,4},{1,5},{2,6},{3,7},{4,0},{5,1},{6,2},{7,3},{8,12},{9,13},{10,... | collective-permute-start | bytes 1572872 | tf_op jit(solution)/shard_map/ppermute | solution.py:34
  49.5 3.1 %collective-permute-start.4 = (bf16[2,3,512]{2,1,0:T(4,128)(2,1)S(1)}, bf16[2,3,512]{2,1,0:T(4,128)(2,1)S(1)}, u32[]{:S(2)}, u32[]{:S(2)}) collective-permute-start(bf16[2,3,512]{2,1,0:T(4,128)(2,1)S(1)} %pad_maximum_fusion.2), channel_id=1, source_target_pairs={{16,0},{32,16},{48,32},{64,48},{80,64},{96,80},{112,96},{128,112},... | collective-permute-start | bytes 18440 | tf_op jit(solution)/shard_map/ppermute | solution.py:14
  52.8 3.8 %collective-permute-done.2 = bf16[2,2,1,256,256]{4,3,1,0,2:T(8,128)(2,1)S(1)} collective-permute-done((bf16[2,2,1,256,256]{4,3,1,0,2:T(8,128)(2,1)S(1)}, bf16[2,2,1,256,256]{4,3,1,0,2:T(8,128)(2,1)S(1)}, u32[]{:S(2)}, u32[]{:S(2)}) %collective-permute-start.2) | collective-permute-done | bytes 524320 | tf_op jit(solution)/shard_map/ppermute | solution.py:34
  56.7 1.9 %collective-permute-start.3 = (bf16[2,2,2,1,256,256]{5,4,2,0,1,3:T(8,128)(2,1)S(1)}, bf16[2,2,2,1,256,256]{5,4,2,0,1,3:T(8,128)(2,1)}, u32[]{:S(2)}, u32[]{:S(2)}) collective-permute-start(bf16[2,2,2,1,256,256]{5,4,2,0,1,3:T(8,128)(2,1)S(1)} %bitcast_dynamic-update-slice_fusion.3), channel_id=1, source_target_pairs={{0,1},{1,0},{2,3},{3,2},{4,5},{5,4},{6,7},{7,6},{8,9},{9,8},{10,11... | collective-permute-start | bytes 3145736 | tf_op jit(solution)/shard_map/ppermute | solution.py:34
  59.2 1.2 multiply_reduce_fusion.1
  60.5 3.1 %collective-permute-start.6 = (f32[5,512]{1,0:T(8,128)S(1)}, f32[5,512]{1,0:T(8,128)S(1)}, u32[]{:S(2)}, u32[]{:S(2)}) collective-permute-start(f32[5,512]{1,0:T(8,128)S(1)} %concatenate.22), channel_id=1, source_target_pairs={{0,16},{16,0},{32,48},{48,32},{64,80},{80,64},{96,112},{112,96},{1... | collective-permute-start | bytes 30728 | tf_op jit(solution)/shard_map/ppermute | solution.py:25
  63.6 2.5 %collective-permute-done.6 = f32[5,512]{1,0:T(8,128)S(1)} collective-permute-done((f32[5,512]{1,0:T(8,128)S(1)}, f32[5,512]{1,0:T(8,128)S(1)}, u32[]{:S(2)}, u32[]{:S(2)}) %collective-permute-start.6) | collective-permute-done | bytes 10272 | tf_op jit(solution)/shard_map/ppermute | solution.py:25
  66.1 4.6 %collective-permute-start.7 = (f32[5,512]{1,0:T(8,128)S(1)}, f32[5,512]{1,0:T(8,128)S(1)}, u32[]{:S(2)}, u32[]{:S(2)}) collective-permute-start(f32[5,512]{1,0:T(8,128)S(1)} %add.106), channel_id=1, source_target_pairs={{0,32},{16,48},{32,0},{48,16},{64,96},{80,112},{96,64},{112,80},{1... | collective-permute-start | bytes 30728 | tf_op jit(solution)/shard_map/ppermute | solution.py:25
  70.7 2.7 %collective-permute-done.7 = f32[5,512]{1,0:T(8,128)S(1)} collective-permute-done((f32[5,512]{1,0:T(8,128)S(1)}, f32[5,512]{1,0:T(8,128)S(1)}, u32[]{:S(2)}, u32[]{:S(2)}) %collective-permute-start.7) | collective-permute-done | bytes 10272 | tf_op jit(solution)/shard_map/ppermute | solution.py:25
  73.5 1.9 %collective-permute-start.8 = (f32[5,512]{1,0:T(8,128)S(1)}, f32[5,512]{1,0:T(8,128)S(1)}, u32[]{:S(2)}, u32[]{:S(2)}) collective-permute-start(f32[5,512]{1,0:T(8,128)S(1)} %add.107), channel_id=1, source_target_pairs={{0,64},{16,80},{32,96},{48,112},{64,0},{80,16},{96,32},{112,48},{1... | collective-permute-start | bytes 30728 | tf_op jit(solution)/shard_map/ppermute | solution.py:25
  75.4 5.5 %collective-permute-done.8 = f32[5,512]{1,0:T(8,128)S(1)} collective-permute-done((f32[5,512]{1,0:T(8,128)S(1)}, f32[5,512]{1,0:T(8,128)S(1)}, u32[]{:S(2)}, u32[]{:S(2)}) %collective-permute-start.8) | collective-permute-done | bytes 10272 | tf_op jit(solution)/shard_map/ppermute | solution.py:25
  80.9 4.3 %collective-permute-start.9 = (f32[5,512]{1,0:T(8,128)S(1)}, f32[5,512]{1,0:T(8,128)S(1)}, u32[]{:S(2)}, u32[]{:S(2)}) collective-permute-start(f32[5,512]{1,0:T(8,128)S(1)} %add.108), channel_id=1, source_target_pairs={{0,128},{16,144},{32,160},{48,176},{64,192},{80,208},{96,224},{112... | collective-permute-start | bytes 30728 | tf_op jit(solution)/shard_map/ppermute | solution.py:25
  85.2 5.6 %collective-permute-done.9 = f32[5,512]{1,0:T(8,128)S(1)} collective-permute-done((f32[5,512]{1,0:T(8,128)S(1)}, f32[5,512]{1,0:T(8,128)S(1)}, u32[]{:S(2)}, u32[]{:S(2)}) %collective-permute-start.9) | collective-permute-done | bytes 10272 | tf_op jit(solution)/shard_map/ppermute | solution.py:25
  90.8 12.7 %collective-permute-start.10 = (f32[5,512]{1,0:T(8,128)S(1)}, f32[5,512]{1,0:T(8,128)S(1)}, u32[]{:S(2)}, u32[]{:S(2)}) collective-permute-start(f32[5,512]{1,0:T(8,128)S(1)} %add.109), channel_id=1, source_target_pairs={{0,256},{16,272},{32,288},{48,304},{64,320},{80,336},{96,352},{112... | collective-permute-start | bytes 30728 | tf_op jit(solution)/shard_map/ppermute | solution.py:25
  103.5 3.4 %collective-permute-done.10 = f32[5,512]{1,0:T(8,128)S(1)} collective-permute-done((f32[5,512]{1,0:T(8,128)S(1)}, f32[5,512]{1,0:T(8,128)S(1)}, u32[]{:S(2)}, u32[]{:S(2)}) %collective-permute-start.10) | collective-permute-done | bytes 10272 | tf_op jit(solution)/shard_map/ppermute | solution.py:25
  106.9 20.9 %collective-permute-start.11 = (f32[5,512]{1,0:T(8,128)S(1)}, f32[5,512]{1,0:T(8,128)S(1)}, u32[]{:S(2)}, u32[]{:S(2)}) collective-permute-start(f32[5,512]{1,0:T(8,128)S(1)} %add.110), channel_id=1, source_target_pairs={{0,512},{16,528},{32,544},{48,560},{64,576},{80,592},{96,608},{112... | collective-permute-start | bytes 30728 | tf_op jit(solution)/shard_map/ppermute | solution.py:25
  127.8 3.6 %collective-permute-done.11 = f32[5,512]{1,0:T(8,128)S(1)} collective-permute-done((f32[5,512]{1,0:T(8,128)S(1)}, f32[5,512]{1,0:T(8,128)S(1)}, u32[]{:S(2)}, u32[]{:S(2)}) %collective-permute-start.11) | collective-permute-done | bytes 10272 | tf_op jit(solution)/shard_map/ppermute | solution.py:25
  131.4 0.6 slice.106
  132.0 0.6 slice.107
  132.9 1.3 bitcast_dynamic-update-slice_fusion.1
  134.2 2.4 %copy.16 = bf16[256,16,256]{0,2,1:T(8,128)(2,1)} copy(bf16[256,16,256]{2,0,1:T(8,128)(2,1)S(1)} %bitcast.49) | data formatting | bytes 4194304 | tf_op jit(solution)/shard_map/transpose | solution.py:75
  136.6 25.2 %all-gather.2.cloned.1.call-done = bf16[512,4096]{1,0:T(8,128)(2,1)} async-done(((bf16[32,4096]{1,0:T(8,128)(2,1)}), bf16[512,4096]{1,0:T(8,128)(2,1)}) %all-gather.2.cloned.1.call-update) | async-done | bytes 4194320 | tf_op jit(solution)/shard_map/all_gather | solution.py:74
  161.8 5.0 %fusion.8 = (bf16[256,512]{1,0:T(8,128)(2,1)}, bf16[256,512]{1,0:T(8,128)(2,1)}) fusion(bf16[256,512]{1,0:T(8,128)(2,1)S(1)} %copy-done.4, bf16[256,512]{1,0:T(8,128)(2,1)S(1)} %copy-done.5, bf16[256,4096]{0,1:T(8,128)(2,1)} %bitcast.50, bf16[512,4096]{1,0:T(8,128)(2,1)} %all-gather.2.cloned.1.call-done), kind=kOutput, calls=%fused_computation.18 | convolution fusion | flops 1075707904 | bytes 7340032 | tf_op jit(solution)/shard_map/dot_general | solution.py:76
  (39 shorter events, 1.3 us)
Async XLA Ops:
  7.2 45.5 %copy-start.2 = (f32[4,512]{1,0:T(4,128)S(1)}, f32[4,512]{1,0:T(4,128)}, u32[]{:S(2)}) copy-start(f32[4,512]{1,0:T(4,128)} %param.14) | copy-start | bytes 24580
  7.2 154.6 %all-gather.2.cloned.1.call-start = ((), (), s32[]{:S(2)}) async-start(), calls=%async_computation | async-start | bytes 4456448 | tf_op jit(solution)/shard_map/all_gather | solution.py:74
  20.6 8.6 %collective-permute-start = (bf16[1,256,256]{2,1,0:T(8,128)(2,1)}, bf16[1,256,256]{2,1,0:T(8,128)(2,1)S(1)}, u32[]{:S(2)}, u32[]{:S(2)}) collective-permute-start(bf16[1,256,256]{2,1,0:T(8,128)(2,1)} %bitcast.51), channel_id=1, source_target_pairs={{0,2},{1,3},{2,0},{3,1},{4,6},{5,7},{6,4},{7,5},{8,10},{9,11},{10,... | collective-permute-start | bytes 393224 | tf_op jit(solution)/shard_map/ppermute | solution.py:34
  24.5 34.1 %collective-permute-start.5 = (bf16[3,512]{1,0:T(4,128)(2,1)S(1)}, bf16[3,512]{1,0:T(4,128)(2,1)S(1)}, u32[]{:S(2)}, u32[]{:S(2)}) collective-permute-start(bf16[3,512]{1,0:T(4,128)(2,1)S(1)} %get-tuple-element.14), channel_id=1, source_target_pairs={{0,16},{16,32},{32,48},{48,64},{64,80},{80,96},{96,112},{112,128},... | collective-permute-start | bytes 9224 | tf_op jit(solution)/shard_map/ppermute | solution.py:14
  29.2 9.8 %collective-permute-start.1 = (bf16[2,1,256,256]{3,2,0,1:T(8,128)(2,1)S(1)}, bf16[2,1,256,256]{3,2,0,1:T(8,128)(2,1)S(1)}, u32[]{:S(2)}, u32[]{:S(2)}) collective-permute-start(bf16[2,1,256,256]{3,2,0,1:T(8,128)(2,1)S(1)} %bitcast_dynamic-update-slice_fusion.6), channel_id=1, source_target_pairs={{0,8},{1,9},{2,10},{3,11},{4,12},{5,13},{6,14},{7,15},{8,0},{9,1},... | collective-permute-start | bytes 786440 | tf_op jit(solution)/shard_map/ppermute | solution.py:34
  33.3 25.4 %copy-start = (bf16[256,512]{1,0:T(8,128)(2,1)S(1)}, bf16[256,512]{1,0:T(8,128)(2,1)}, u32[]{:S(2)}) copy-start(bf16[256,512]{1,0:T(8,128)(2,1)} %param.12) | copy-start | bytes 786436
  33.3 25.4 %copy-start.1 = (bf16[256,512]{1,0:T(8,128)(2,1)S(1)}, bf16[256,512]{1,0:T(8,128)(2,1)}, u32[]{:S(2)}) copy-start(bf16[256,512]{1,0:T(8,128)(2,1)} %param.13) | copy-start | bytes 786436
  33.4 25.4 %copy-start.3 = (f32[512]{0:T(512)S(1)}, f32[512]{0:T(512)}, u32[]{:S(2)}) copy-start(f32[512]{0:T(512)} %param.15) | copy-start | bytes 6148
  39.0 17.6 %collective-permute-start.2 = (bf16[2,2,1,256,256]{4,3,1,0,2:T(8,128)(2,1)S(1)}, bf16[2,2,1,256,256]{4,3,1,0,2:T(8,128)(2,1)S(1)}, u32[]{:S(2)}, u32[]{:S(2)}) collective-permute-start(bf16[2,2,1,256,256]{4,3,1,0,2:T(8,128)(2,1)S(1)} %bitcast_dynamic-update-slice_fusion.5), channel_id=1, source_target_pairs={{0,4},{1,5},{2,6},{3,7},{4,0},{5,1},{6,2},{7,3},{8,12},{9,13},{10,... | collective-permute-start | bytes 1572872 | tf_op jit(solution)/shard_map/ppermute | solution.py:34
  49.5 9.1 %collective-permute-start.4 = (bf16[2,3,512]{2,1,0:T(4,128)(2,1)S(1)}, bf16[2,3,512]{2,1,0:T(4,128)(2,1)S(1)}, u32[]{:S(2)}, u32[]{:S(2)}) collective-permute-start(bf16[2,3,512]{2,1,0:T(4,128)(2,1)S(1)} %pad_maximum_fusion.2), channel_id=1, source_target_pairs={{16,0},{32,16},{48,32},{64,48},{80,64},{96,80},{112,96},{128,112},... | collective-permute-start | bytes 18440 | tf_op jit(solution)/shard_map/ppermute | solution.py:14
  56.7 76.2 %collective-permute-start.3 = (bf16[2,2,2,1,256,256]{5,4,2,0,1,3:T(8,128)(2,1)S(1)}, bf16[2,2,2,1,256,256]{5,4,2,0,1,3:T(8,128)(2,1)}, u32[]{:S(2)}, u32[]{:S(2)}) collective-permute-start(bf16[2,2,2,1,256,256]{5,4,2,0,1,3:T(8,128)(2,1)S(1)} %bitcast_dynamic-update-slice_fusion.3), channel_id=1, source_target_pairs={{0,1},{1,0},{2,3},{3,2},{4,5},{5,4},{6,7},{7,6},{8,9},{9,8},{10,11... | collective-permute-start | bytes 3145736 | tf_op jit(solution)/shard_map/ppermute | solution.py:34
  60.5 5.6 %collective-permute-start.6 = (f32[5,512]{1,0:T(8,128)S(1)}, f32[5,512]{1,0:T(8,128)S(1)}, u32[]{:S(2)}, u32[]{:S(2)}) collective-permute-start(f32[5,512]{1,0:T(8,128)S(1)} %concatenate.22), channel_id=1, source_target_pairs={{0,16},{16,0},{32,48},{48,32},{64,80},{80,64},{96,112},{112,96},{1... | collective-permute-start | bytes 30728 | tf_op jit(solution)/shard_map/ppermute | solution.py:25
  66.1 7.3 %collective-permute-start.7 = (f32[5,512]{1,0:T(8,128)S(1)}, f32[5,512]{1,0:T(8,128)S(1)}, u32[]{:S(2)}, u32[]{:S(2)}) collective-permute-start(f32[5,512]{1,0:T(8,128)S(1)} %add.106), channel_id=1, source_target_pairs={{0,32},{16,48},{32,0},{48,16},{64,96},{80,112},{96,64},{112,80},{1... | collective-permute-start | bytes 30728 | tf_op jit(solution)/shard_map/ppermute | solution.py:25
  73.5 7.4 %collective-permute-start.8 = (f32[5,512]{1,0:T(8,128)S(1)}, f32[5,512]{1,0:T(8,128)S(1)}, u32[]{:S(2)}, u32[]{:S(2)}) collective-permute-start(f32[5,512]{1,0:T(8,128)S(1)} %add.107), channel_id=1, source_target_pairs={{0,64},{16,80},{32,96},{48,112},{64,0},{80,16},{96,32},{112,48},{1... | collective-permute-start | bytes 30728 | tf_op jit(solution)/shard_map/ppermute | solution.py:25
  80.9 9.9 %collective-permute-start.9 = (f32[5,512]{1,0:T(8,128)S(1)}, f32[5,512]{1,0:T(8,128)S(1)}, u32[]{:S(2)}, u32[]{:S(2)}) collective-permute-start(f32[5,512]{1,0:T(8,128)S(1)} %add.108), channel_id=1, source_target_pairs={{0,128},{16,144},{32,160},{48,176},{64,192},{80,208},{96,224},{112... | collective-permute-start | bytes 30728 | tf_op jit(solution)/shard_map/ppermute | solution.py:25
  90.8 16.1 %collective-permute-start.10 = (f32[5,512]{1,0:T(8,128)S(1)}, f32[5,512]{1,0:T(8,128)S(1)}, u32[]{:S(2)}, u32[]{:S(2)}) collective-permute-start(f32[5,512]{1,0:T(8,128)S(1)} %add.109), channel_id=1, source_target_pairs={{0,256},{16,272},{32,288},{48,304},{64,320},{80,336},{96,352},{112... | collective-permute-start | bytes 30728 | tf_op jit(solution)/shard_map/ppermute | solution.py:25
  106.9 24.5 %collective-permute-start.11 = (f32[5,512]{1,0:T(8,128)S(1)}, f32[5,512]{1,0:T(8,128)S(1)}, u32[]{:S(2)}, u32[]{:S(2)}) collective-permute-start(f32[5,512]{1,0:T(8,128)S(1)} %add.110), channel_id=1, source_target_pairs={{0,512},{16,528},{32,544},{48,560},{64,576},{80,592},{96,608},{112... | collective-permute-start | bytes 30728 | tf_op jit(solution)/shard_map/ppermute | solution.py:25
  134.2 27.6 %copy-start.4 = (bf16[256,512]{1,0:T(8,128)(2,1)S(1)}, bf16[256,512]{1,0:T(8,128)(2,1)}, u32[]{:S(2)}) copy-start(bf16[256,512]{1,0:T(8,128)(2,1)} %param.11) | copy-start | bytes 786436
  134.2 27.6 %copy-start.5 = (bf16[256,512]{1,0:T(8,128)(2,1)S(1)}, bf16[256,512]{1,0:T(8,128)(2,1)}, u32[]{:S(2)}) copy-start(bf16[256,512]{1,0:T(8,128)(2,1)} %param.10) | copy-start | bytes 786436
Sparse Core Ops, SparseCore 0:
  20.8 140.9 all-gather.1
